TPU v7x, 256 devices: a whole 4x4x8 slice. The times are simulated.
256 devices in a mesh: leaf: 32 (over x, z), basis: 2 (over core), coup: 4 (over y).
Axes of the slice: x: 4, y: 4, z: 8, core: 2. Of those that a mesh axis runs over, the one named last changes fastest.
Arguments:
- basis_rows: bfloat16 [2048, 131072], P('leaf', ('basis', 'coup')), may hold values from -0.125 to 0.125
- transfer: bfloat16 [3072, 4096], P('leaf'), may hold values from -0.5 to 0.5
- omega: bfloat16 [3584, 2048], P('leaf'), may hold values from -0.75 to 0.75
- blocks: bfloat16 [196608, 4096], P(('leaf', 'basis', 'coup')), may hold values from -6 to 6
- block_target: int32 [196608], P(('leaf', 'basis', 'coup')), may hold values from 0 to 111
- source_leaf: int32 [196608, 1], P(('leaf', 'basis', 'coup')), may hold values from 0 to 31; in each aligned block of 768 rows (0 to 767, 768 to 1535, ...) at most 36 rows name the same one
- source_offset: int32 [196608], P(('leaf', 'basis', 'coup')), may hold values from 0 to 63
Outputs:
- projected: float32 [196608, 1024], P(('leaf', 'basis', 'coup'))
Inputs may be any that keep to these rules, and one draw needn't show every extreme that they name: `source_leaf`: among the 768 rows of one device, no branch is named by more than 36 rows, a bound that some block reaches.
All inputs are finite; a program needn't handle non-finite values.
Results may differ from a plain program's by a relative error of at most 0.0049.
Values may be sent and summed in bfloat16 or wider, within the bound.
No kernel may reach another device: no remote copies, remote signals or barrier semaphores. Data moves between devices by JAX's collectives and lax.ppermute only.
A program may use at most 128 MiB of HBM per device.

v0:
```python
import jax
import jax.numpy as jnp
from jax import lax
from jax.sharding import PartitionSpec as P

K = 64
R = 32
NB = 64


def level_slots(target):
    base = jnp.where(target < NB, 0, jnp.where(target < NB + NB // 2, NB, NB + NB // 2))
    node_count = jnp.where(target < NB, NB, jnp.where(target < NB + NB // 2, NB // 2, NB // 4))
    return (base, node_count)


def upsweep(gram_bottom, transfer, omega, bottom_count):
    links = transfer.reshape(-1, K, K).astype(jnp.float32)
    levels = [gram_bottom]
    gram_now = gram_bottom
    offset_row = 0
    for node_count in (bottom_count, bottom_count // 2):
        child_links = links[offset_row : offset_row + node_count]
        offset_row = offset_row + node_count
        carried = jnp.einsum(
            "nki,nkl,nlj->nij", child_links, gram_now, child_links, precision=lax.Precision.HIGHEST
        )
        gram_now = carried.reshape(node_count // 2, 2, K, K).sum(axis=1)
        levels.append(gram_now)
    gram_all = jnp.concatenate(levels, axis=0)
    factor = jnp.linalg.cholesky(gram_all)
    sketch = omega.reshape(-1, K, R).astype(jnp.float32)
    basis_table = jnp.einsum("nkr,njk->nrj", sketch, factor, precision=lax.Precision.HIGHEST)
    return basis_table.astype(jnp.bfloat16).reshape(-1, R * K)


def project(target_rows, source_rows, coupling):
    target_mat = target_rows.reshape(-1, R, K)
    coupling_mat = coupling.reshape(-1, K, K)
    left_prod = jnp.einsum(
        "brk,bkl->brl", target_mat, coupling_mat, preferred_element_type=jnp.float32
    ).astype(jnp.bfloat16)
    source_mat = source_rows.reshape(-1, R, K)
    result = jnp.einsum("brl,bjl->brj", left_prod, source_mat, preferred_element_type=jnp.float32)
    return result.reshape(-1, R * R)


def per_device(basis_rows, transfer, omega, blocks, block_target, source_leaf, source_offset):
    rows_local = basis_rows.reshape(NB, -1, K)
    partial_gram = jnp.einsum(
        "nik,nil->nkl", rows_local, rows_local, preferred_element_type=jnp.float32
    )
    gram_share = lax.psum_scatter(partial_gram, ("basis", "coup"), scatter_dimension=0, tiled=True)
    group = lax.axis_size(("basis", "coup"))
    member = lax.axis_index(("basis", "coup"))
    local_count = NB // group
    half_count = local_count // 2
    quarter_count = local_count // 4
    links_local = jnp.concatenate(
        [
            lax.dynamic_slice_in_dim(transfer, member * local_count, local_count, 0),
            lax.dynamic_slice_in_dim(transfer, NB + member * half_count, half_count, 0),
        ],
        axis=0,
    )
    sketch_local = jnp.concatenate(
        [
            lax.dynamic_slice_in_dim(omega, member * local_count, local_count, 0),
            lax.dynamic_slice_in_dim(omega, NB + member * half_count, half_count, 0),
            lax.dynamic_slice_in_dim(
                omega, NB + NB // 2 + member * quarter_count, quarter_count, 0
            ),
        ],
        axis=0,
    )
    local_table = upsweep(gram_share, links_local, sketch_local, local_count)
    collected = lax.all_gather(local_table, ("basis", "coup"), axis=0, tiled=True)
    collected = collected.reshape(group, local_count + half_count + quarter_count, R * K)
    basis_table = jnp.concatenate(
        [
            collected[:, :local_count].reshape(-1, R * K),
            collected[:, local_count : local_count + half_count].reshape(-1, R * K),
            collected[:, local_count + half_count :].reshape(-1, R * K),
        ],
        axis=0,
    )
    slots_per_leaf = basis_table.shape[0]
    base, node_count = level_slots(block_target)
    source_slot = base + source_offset % node_count
    source_peer = source_leaf[:, 0]
    gathered = lax.all_gather(basis_table, "leaf", axis=0, tiled=True)
    source_rows = gathered[source_peer * slots_per_leaf + source_slot]
    return project(basis_table[block_target], source_rows, blocks)


def solution(mesh):
    placed = (
        P("leaf", ("basis", "coup")),
        P("leaf", None),
        P("leaf", None),
        P(("leaf", "basis", "coup"), None),
        P(("leaf", "basis", "coup")),
        P(("leaf", "basis", "coup"), None),
        P(("leaf", "basis", "coup")),
    )
    return jax.shard_map(
        per_device,
        mesh=mesh,
        in_specs=placed,
        out_specs=P(("leaf", "basis", "coup"), None),
        check_vma=False,
    )
```

profile of v0, /device:TPU:1, one launch (start us, length us, event | category | flops | bytes accessed | tf_op | source)
XLA Modules:
  0.0 368.6 jit_solution(15794616053959526553)
XLA Ops:
  6.5 0.0 copy-start
  6.5 0.0 reduce-scatter.2.cloned.1.call-start
  6.5 6.5 %reshape.50 = bf16[64,256,64]{2,1,0:T(8,128)(2,1)} reshape(bf16[64,16384]{1,0:T(8,128)(2,1)} %param.7) | data formatting | bytes 4194304 | tf_op jit(solution)/shard_map/reshape | solution.py:49
  13.1 6.3 %fusion.16 = f32[64,64,64]{1,2,0:T(8,128)} fusion(bf16[64,256,64]{2,1,0:T(8,128)(2,1)} %reshape.50), kind=kOutput, calls=%fused_computation.41 | convolution fusion | flops 134217728 | bytes 3145728 | tf_op jit(solution)/shard_map/nik,nil->nkl/dot_general | solution.py:50
  19.4 0.0 reduce-scatter.2.cloned.1.call-update
  19.4 0.0 all-gather.3.cloned.1.call-start
  19.5 0.0 copy-done
  19.5 0.1 slice.24
  19.7 0.2 slice.23
  19.8 0.8 constant_dynamic-slice_fusion.2
  20.6 0.8 constant_dynamic-slice_fusion.3
  21.4 0.8 constant_dynamic-slice_fusion.4
  22.2 0.2 reshape.49
  22.4 41.6 %reduce-scatter.2.cloned.1.call-done = f32[8,64,64]{1,2,0:T(8,128)} async-done(((f32[64,64,64]{1,2,0:T(8,128)}), f32[8,64,64]{1,2,0:T(8,128)}) %reduce-scatter.2.cloned.1.call-update) | async-done | bytes 131088 | tf_op jit(solution)/shard_map/reduce_scatter | solution.py:53
  64.0 1.3 fusion.17
  65.3 0.3 bitcast_reduce_fusion
  65.6 0.1 copy.47
  65.7 0.3 fusion.18
  65.9 0.2 bitcast_reduce_fusion.1
  66.1 0.1 copy.48
  66.2 1.0 pad_maximum_fusion
  67.2 0.2 copy.49
  67.4 1.0 fusion.4
  68.4 82.1 %custom-call.4 = f32[14,64,64]{2,1,0:T(8,128)S(1)} custom-call(f32[14,64,64]{2,1,0:T(8,128)S(1)} %fusion.4), custom_call_target="Cholesky" | custom-call | tf_op jit(solution)/shard_map/jit(cholesky)/cholesky | solution.py:31
  150.5 0.1 select_reduce_fusion
  150.5 0.1 compare_reduce_fusion
  150.7 0.6 convolution_convert_fusion
  151.2 0.2 reshape.80
  151.4 23.2 %all-gather = bf16[8,14,2048]{2,1,0:T(8,128)(2,1)S(1)} all-gather(bf16[1,14,2048]{2,1,0:T(8,128)(2,1)S(1)} %reshape.80), channel_id=1, replica_groups=mesh['leaf'=32,'basis'=2,'coup'=4] {'basis','coup'}, dimensions={0}, use_global_device_ids=true | all-gather | bytes 516096 | tf_op jit(solution)/shard_map/all_gather | solution.py:77
  174.6 0.1 slice.34
  174.8 0.8 pad_maximum_fusion.1
  175.6 0.0 all-gather.3.cloned.1.call-update
  175.6 8.7 %copy.52 = bf16[768,4096]{0,1:T(8,128)(2,1)} copy(bf16[768,4096]{1,0:T(8,128)(2,1)} %param.10) | data formatting | bytes 12582912 | tf_op args[3]
  184.3 0.0 copy-start.5
  184.3 0.0 copy-start.3
  184.3 0.0 copy-start.4
  184.3 0.0 copy-start.2
  184.3 18.5 %copy.54 = bf16[768,64,64]{2,1,0:T(8,128)(2,1)} copy(bf16[768,64,64]{0,2,1:T(8,128)(2,1)} %bitcast.28) | data formatting | bytes 12582912 | tf_op jit(solution)/shard_map/reshape | solution.py:39
  202.9 0.0 copy-done.5
  202.9 0.0 copy-done.3
  202.9 0.0 copy-done.4
  202.9 0.1 compare_select_fusion.2
  203.0 0.0 copy-done.2
  203.1 4.2 %gather_fusion = bf16[768,2048]{1,0:T(8,128)(2,1)} fusion(bf16[112,2048]{1,0:T(8,128)(2,1)S(1)} %copy-done.2, s32[1024]{0:T(1024)S(1)} %pad_clamp_fusion.1), kind=kCustom, calls=%fused_computation | custom fusion | bytes 6294528 | tf_op jit(solution)/shard_map/gather | solution.py:93
  207.3 4.7 %copy.51 = bf16[768,2048]{0,1:T(8,128)(2,1)} copy(bf16[768,2048]{1,0:T(8,128)(2,1)} %gather_fusion) | data formatting | bytes 6291456 | tf_op jit(solution)/shard_map/gather | solution.py:93
  212.0 10.2 %copy.53 = bf16[768,32,64]{2,1,0:T(8,128)(2,1)} copy(bf16[768,32,64]{0,2,1:T(8,128)(2,1)} %bitcast.29) | data formatting | bytes 6291456 | tf_op jit(solution)/shard_map/reshape | solution.py:38
  222.2 82.1 %all-gather.3.cloned.1.call-done = bf16[3584,2048]{1,0:T(8,128)(2,1)} async-done(((bf16[112,2048]{1,0:T(8,128)(2,1)}), bf16[3584,2048]{1,0:T(8,128)(2,1)}) %all-gather.3.cloned.1.call-update) | async-done | bytes 14680080 | tf_op jit(solution)/shard_map/all_gather | solution.py:91
  304.3 14.1 %gather_fusion.1 = bf16[768,2048]{1,0:T(8,128)(2,1)} fusion(bf16[3584,2048]{1,0:T(8,128)(2,1)} %all-gather.3.cloned.1.call-done, s32[1024]{0:T(1024)S(1)} %pad_clamp_fusion), kind=kCustom, calls=%fused_computation.1 | custom fusion | bytes 6294528 | tf_op jit(solution)/shard_map/gather | solution.py:92
  318.5 4.7 %copy.55 = bf16[768,2048]{0,1:T(8,128)(2,1)} copy(bf16[768,2048]{1,0:T(8,128)(2,1)} %gather_fusion.1) | data formatting | bytes 6291456 | tf_op jit(solution)/shard_map/gather | solution.py:92
  323.1 10.2 %copy.56 = bf16[768,32,64]{2,1,0:T(8,128)(2,1)} copy(bf16[768,32,64]{0,2,1:T(8,128)(2,1)} %bitcast.30) | data formatting | bytes 6291456 | tf_op jit(solution)/shard_map/reshape | solution.py:43
  333.3 14.4 %fusion = f32[768,32,32]{2,1,0:T(8,128)} fusion(bf16[768,32,64]{2,1,0:T(8,128)(2,1)} %copy.56, bf16[768,32,64]{2,1,0:T(8,128)(2,1)} %copy.53, bf16[768,64,64]{2,1,0:T(8,128)(2,1)} %copy.54), kind=kOutput, calls=%fused_computation.2 | convolution fusion | flops 303562752 | bytes 15728640 | tf_op jit(solution)/shard_map/brl,bjl->brj/dot_general | solution.py:44
  347.7 0.0 copy-start.1
  347.7 10.5 %copy.57 = f32[768,32,32]{0,2,1:T(8,128)} copy(f32[768,32,32]{2,1,0:T(8,128)} %fusion) | data formatting | bytes 6291456 | tf_op jit(solution)/shard_map/brl,bjl->brj/dot_general | solution.py:44
  358.2 3.5 copy.58
  361.8 0.0 copy-done.1
  (12 shorter events, 0.2 us)
Async XLA Ops:
  6.5 12.9 %copy-start = (bf16[96,4096]{1,0:T(8,128)(2,1)S(1)}, bf16[96,4096]{1,0:T(8,128)(2,1)}, u32[]{:S(2)}) copy-start(bf16[96,4096]{1,0:T(8,128)(2,1)} %param.8) | copy-start | bytes 2359300
  6.5 57.4 %reduce-scatter.2.cloned.1.call-start = ((), (), s32[]{:S(2)}) async-start(), calls=%async_computation.1 | async-start | bytes 2359296 | tf_op jit(solution)/shard_map/reduce_scatter | solution.py:53
  19.4 284.9 %all-gather.3.cloned.1.call-start = ((), (), s32[]{:S(2)}) async-start(), calls=%async_computation.2 | async-start | bytes 15138816 | tf_op jit(solution)/shard_map/all_gather | solution.py:91
  184.3 18.5 %copy-start.5 = (s32[768,1]{0,1:T(1,128)S(1)}, s32[768,1]{0,1:T(1,128)}, u32[]{:S(2)}) copy-start(s32[768,1]{0,1:T(1,128)} %param.12) | copy-start | bytes 9220
  184.3 18.5 %copy-start.3 = (s32[768]{0:T(1024)S(1)}, s32[768]{0:T(1024)}, u32[]{:S(2)}) copy-start(s32[768]{0:T(1024)} %param.11) | copy-start | bytes 9220
  184.3 18.5 %copy-start.4 = (s32[768]{0:T(1024)S(1)}, s32[768]{0:T(1024)}, u32[]{:S(2)}) copy-start(s32[768]{0:T(1024)} %param.13) | copy-start | bytes 9220
  184.3 18.7 %copy-start.2 = (bf16[112,2048]{1,0:T(8,128)(2,1)S(1)}, bf16[112,2048]{1,0:T(8,128)(2,1)}, u32[]{:S(2)}) copy-start(bf16[112,2048]{1,0:T(8,128)(2,1)} %pad_maximum_fusion.1) | copy-start | bytes 1376260
  347.7 14.0 %copy-start.1 = (bf16[96,4096]{1,0:T(8,128)(2,1)S(1)}, bf16[96,4096]{1,0:T(8,128)(2,1)}, u32[]{:S(2)}) copy-start(bf16[96,4096]{1,0:T(8,128)(2,1)} %param.8) | copy-start | bytes 2359300
Sparse Core Ops, SparseCore 0:
  19.5 44.3 reduce-scatter.1
  175.8 128.5 all-gather.2
where the time goes:
time: 370 us; the launch traced here: 369 us
  waiting for transfers between devices  124 us (34%)
  local copies, waits for them, and re-layouts  99.5 us (27%)
  other arithmetic  85.3 us (23%)
  matrix products  23.3 us (6%)
  blocking collectives  23.2 us (6%)
  between operations  13.6 us (4%)
    another operation x4, other arithmetic, upsweep(): factor = jnp.linalg.cholesky(gram_all)  82.2 us
    all_gather x1, waiting for transfers between devices, per_device(): gathered = lax.all_gather(basis_table, 'leaf', axis=0, tiled=True)  82.1 us
    reduce_scatter x1, waiting for transfers between devices, per_device(): lax.psum_scatter(partial_gram, ('basis', 'coup'), scatter_dimension=0, ti...  41.6 us
    all_gather x1, blocking collectives, per_device(): lax.all_gather(local_table, ('basis', 'coup'), axis=0, tiled=True)  23.2 us
    gather x2, local copies, waits for them, and re-layouts, per_device(): source_rows = gathered[source_peer * slots_per_leaf + source_slot]  18.8 us
    reshape x1, local copies, waits for them, and re-layouts, project(): coupling_mat = coupling.reshape(-1, K, K)  18.5 us
    dot_general x1, matrix products, project(): jnp.einsum('brl,bjl->brj', left_prod, source_mat, preferred_element_type=...  14.4 us
    dot_general x1, local copies, waits for them, and re-layouts, project(): jnp.einsum('brl,bjl->brj', left_prod, source_mat, preferred_element_type=...  10.5 us
  transfers between devices with their start and end apart: 2, of which 2 were waited for; matrix products, arithmetic and copies ran while one was open for 13% of the time, Pallas kernels for 0%

commit v1 on v0

--- a/solution.py
+++ b/solution.py
@@ -2,6 +2,8 @@
 import jax.numpy as jnp
 from jax import lax
 from jax.sharding import PartitionSpec as P
+from jax.experimental import pallas as pl
+from jax.experimental.pallas import tpu as pltpu
 
 K = 64
 R = 32
@@ -28,10 +30,35 @@
         gram_now = carried.reshape(node_count // 2, 2, K, K).sum(axis=1)
         levels.append(gram_now)
     gram_all = jnp.concatenate(levels, axis=0)
-    factor = jnp.linalg.cholesky(gram_all)
-    sketch = omega.reshape(-1, K, R).astype(jnp.float32)
-    basis_table = jnp.einsum("nkr,njk->nrj", sketch, factor, precision=lax.Precision.HIGHEST)
+    sketch_t = omega.reshape(-1, K, R).astype(jnp.float32).transpose(0, 2, 1)
+    basis_table = chol_basis(gram_all, sketch_t)
     return basis_table.astype(jnp.bfloat16).reshape(-1, R * K)
+
+
+def chol_kernel(g_ref, om_ref, out_ref, lt_ref):
+    a = g_ref[...]
+    count = a.shape[0]
+    lane = lax.broadcasted_iota(jnp.int32, (count, 1, K), 2)
+    for j in range(K):
+        row = a[:, j : j + 1, :]
+        inv = 1.0 / jnp.sqrt(row[:, :, j : j + 1])
+        scaled = jnp.where(lane >= j, row * inv, 0.0)
+        lt_ref[:, j : j + 1, :] = scaled
+        col = a[:, :, j : j + 1] * inv
+        a = a - col * scaled
+    out_ref[...] = jnp.einsum(
+        "nrk,nkj->nrj", om_ref[...], lt_ref[...], precision=lax.Precision.HIGHEST,
+        preferred_element_type=jnp.float32,
+    )
+
+
+def chol_basis(gram_all, sketch_t):
+    count = gram_all.shape[0]
+    return pl.pallas_call(
+        chol_kernel,
+        out_shape=jax.ShapeDtypeStruct((count, R, K), jnp.float32),
+        scratch_shapes=[pltpu.VMEM((count, K, K), jnp.float32)],
+    )(gram_all, sketch_t)
 
 
 def project(target_rows, source_rows, coupling):

time: 370 us -> 299 us (0.81)
  other arithmetic: 85.3 us -> 3.72 us
  Pallas kernels: 0 us -> 11.5 us
    another operation x4 -> x0, other arithmetic: 82.2 us -> none  [upsweep(): factor = jnp.linalg.cholesky(gram_all)]
    pallas_call x0 -> x1, Pallas kernels: none -> 11.5 us  [chol_basis(): pl.pallas_call(chol_kernel, out_shape=jax.ShapeDtypeStruct((count, R, K),...]
  transfers between devices with their start and end apart: 2 -> 2, of which waited for: 2 -> 2; matrix products, arithmetic and copies ran while one was open for 13% -> 17% of each run, Pallas kernels for 0% -> 0%
where the time goes in v1:
time: 299 us; the launch traced here: 298 us
  waiting for transfers between devices  123 us (41%)
  local copies, waits for them, and re-layouts  100 us (33%)
  blocking collectives  23.2 us (8%)
  matrix products  22.6 us (8%)
  between operations  13.6 us (5%)
  Pallas kernels  11.5 us (4%)
  other arithmetic  3.72 us (1%)
    all_gather x1, waiting for transfers between devices, per_device(): gathered = lax.all_gather(basis_table, 'leaf', axis=0, tiled=True)  82 us
    reduce_scatter x1, waiting for transfers between devices, per_device(): lax.psum_scatter(partial_gram, ('basis', 'coup'), scatter_dimension=0, ti...  40.6 us
    all_gather x1, blocking collectives, per_device(): lax.all_gather(local_table, ('basis', 'coup'), axis=0, tiled=True)  23.2 us
    gather x2, local copies, waits for them, and re-layouts, per_device(): source_rows = gathered[source_peer * slots_per_leaf + source_slot]  18.8 us
    reshape x1, local copies, waits for them, and re-layouts, project(): coupling_mat = coupling.reshape(-1, K, K)  18.5 us
    dot_general x1, matrix products, project(): jnp.einsum('brl,bjl->brj', left_prod, source_mat, preferred_element_type=...  14.4 us
    pallas_call x1, Pallas kernels, chol_basis(): pl.pallas_call(chol_kernel, out_shape=jax.ShapeDtypeStruct((count, R, K),...  11.5 us
    dot_general x1, local copies, waits for them, and re-layouts, project(): jnp.einsum('brl,bjl->brj', left_prod, source_mat, preferred_element_type=...  10.5 us
  transfers between devices with their start and end apart: 2, of which 2 were waited for; matrix products, arithmetic and copies ran while one was open for 17% of the time, Pallas kernels for 0%

profile of v1, /device:TPU:1, one launch (start us, length us, event | category | flops | bytes accessed | tf_op | source)
XLA Modules:
  0.0 297.5 jit_solution(17845840717744347086)
XLA Ops:
  6.5 0.0 copy-start
  6.5 0.0 reduce-scatter.2.cloned.1.call-start
  6.5 6.5 %reshape.44 = bf16[64,256,64]{2,1,0:T(8,128)(2,1)} reshape(bf16[64,16384]{1,0:T(8,128)(2,1)} %param.7) | data formatting | bytes 4194304 | tf_op jit(solution)/shard_map/reshape | solution.py:76
  13.1 6.3 %fusion.7 = f32[64,64,64]{2,1,0:T(8,128)} fusion(bf16[64,256,64]{2,1,0:T(8,128)(2,1)} %reshape.44), kind=kOutput, calls=%fused_computation.26 | convolution fusion | flops 134217728 | bytes 3145728 | tf_op jit(solution)/shard_map/nik,nil->nkl/dot_general | solution.py:77
  19.4 0.0 reduce-scatter.2.cloned.1.call-update
  19.4 0.2 all-gather.3.cloned.1.call-start
  19.6 0.0 copy-done
  19.7 0.1 slice.18
  19.8 0.2 slice.17
  20.0 0.8 constant_dynamic-slice_fusion
  20.8 0.8 constant_dynamic-slice_fusion.1
  21.6 0.8 constant_dynamic-slice_fusion.2
  22.4 0.2 reshape.56
  22.5 0.9 copy.25
  23.4 40.6 %reduce-scatter.2.cloned.1.call-done = f32[8,64,64]{2,1,0:T(8,128)} async-done(((f32[64,64,64]{2,1,0:T(8,128)}), f32[8,64,64]{2,1,0:T(8,128)}) %reduce-scatter.2.cloned.1.call-update) | async-done | bytes 131088 | tf_op jit(solution)/shard_map/reduce_scatter | solution.py:80
  64.0 1.3 fusion.8
  65.3 0.3 bitcast_reduce_fusion
  65.5 0.3 fusion.9
  65.8 0.2 bitcast_reduce_fusion.1
  66.0 1.8 pad_maximum_fusion.g_ref
  67.8 11.5 %shard_map.73 = f32[14,32,64]{2,1,0:T(8,128)} custom-call(f32[14,64,64]{2,1,0:T(8,128)} %pad_maximum_fusion.g_ref, f32[14,32,64]{2,1,0:T(8,128)} %bitcast.28), custom_call_target="tpu_custom_call" | custom-call | tf_op jit(solution)/shard_map/pallas_call | solution.py:57
  79.3 1.0 convert_element_type.12
  80.2 0.1 reshape.75
  80.4 23.2 %all-gather = bf16[8,14,2048]{2,1,0:T(8,128)(2,1)S(1)} all-gather(bf16[1,14,2048]{2,1,0:T(8,128)(2,1)S(1)} %reshape.75), channel_id=1, replica_groups=mesh['leaf'=32,'basis'=2,'coup'=4] {'basis','coup'}, dimensions={0}, use_global_device_ids=true | all-gather | bytes 516096 | tf_op jit(solution)/shard_map/all_gather | solution.py:104
  103.6 0.1 slice.28
  103.8 0.8 pad_maximum_fusion.1
  104.7 0.0 all-gather.3.cloned.1.call-update
  104.7 8.7 %copy.27 = bf16[768,4096]{0,1:T(8,128)(2,1)} copy(bf16[768,4096]{1,0:T(8,128)(2,1)} %param.10) | data formatting | bytes 12582912 | tf_op args[3]
  113.4 0.0 copy-start.5
  113.4 0.0 copy-start.3
  113.4 0.0 copy-start.4
  113.4 0.0 copy-start.2
  113.4 18.5 %copy.29 = bf16[768,64,64]{2,1,0:T(8,128)(2,1)} copy(bf16[768,64,64]{0,2,1:T(8,128)(2,1)} %bitcast.24) | data formatting | bytes 12582912 | tf_op jit(solution)/shard_map/reshape | solution.py:66
  131.9 0.0 copy-done.5
  131.9 0.0 copy-done.3
  131.9 0.0 copy-done.4
  132.0 0.1 compare_select_fusion.2
  132.1 0.0 copy-done.2
  132.1 4.2 %gather_fusion = bf16[768,2048]{1,0:T(8,128)(2,1)} fusion(bf16[112,2048]{1,0:T(8,128)(2,1)S(1)} %copy-done.2, s32[1024]{0:T(1024)S(1)} %pad_clamp_fusion.1), kind=kCustom, calls=%fused_computation | custom fusion | bytes 6294528 | tf_op jit(solution)/shard_map/gather | solution.py:120
  136.4 4.7 %copy.26 = bf16[768,2048]{0,1:T(8,128)(2,1)} copy(bf16[768,2048]{1,0:T(8,128)(2,1)} %gather_fusion) | data formatting | bytes 6291456 | tf_op jit(solution)/shard_map/gather | solution.py:120
  141.1 10.2 %copy.28 = bf16[768,32,64]{2,1,0:T(8,128)(2,1)} copy(bf16[768,32,64]{0,2,1:T(8,128)(2,1)} %bitcast.25) | data formatting | bytes 6291456 | tf_op jit(solution)/shard_map/reshape | solution.py:65
  151.3 82.0 %all-gather.3.cloned.1.call-done = bf16[3584,2048]{1,0:T(8,128)(2,1)} async-done(((bf16[112,2048]{1,0:T(8,128)(2,1)}), bf16[3584,2048]{1,0:T(8,128)(2,1)}) %all-gather.3.cloned.1.call-update) | async-done | bytes 14680080 | tf_op jit(solution)/shard_map/all_gather | solution.py:118
  233.3 14.1 %gather_fusion.1 = bf16[768,2048]{1,0:T(8,128)(2,1)} fusion(bf16[3584,2048]{1,0:T(8,128)(2,1)} %all-gather.3.cloned.1.call-done, s32[1024]{0:T(1024)S(1)} %pad_clamp_fusion), kind=kCustom, calls=%fused_computation.1 | custom fusion | bytes 6294528 | tf_op jit(solution)/shard_map/gather | solution.py:119
  247.4 4.7 %copy.30 = bf16[768,2048]{0,1:T(8,128)(2,1)} copy(bf16[768,2048]{1,0:T(8,128)(2,1)} %gather_fusion.1) | data formatting | bytes 6291456 | tf_op jit(solution)/shard_map/gather | solution.py:119
  252.1 10.2 %copy.31 = bf16[768,32,64]{2,1,0:T(8,128)(2,1)} copy(bf16[768,32,64]{0,2,1:T(8,128)(2,1)} %bitcast.26) | data formatting | bytes 6291456 | tf_op jit(solution)/shard_map/reshape | solution.py:70
  262.3 14.4 %fusion = f32[768,32,32]{2,1,0:T(8,128)} fusion(bf16[768,32,64]{2,1,0:T(8,128)(2,1)} %copy.31, bf16[768,32,64]{2,1,0:T(8,128)(2,1)} %copy.28, bf16[768,64,64]{2,1,0:T(8,128)(2,1)} %copy.29), kind=kOutput, calls=%fused_computation.2 | convolution fusion | flops 303562752 | bytes 15728640 | tf_op jit(solution)/shard_map/brl,bjl->brj/dot_general | solution.py:71
  276.7 0.0 copy-start.1
  276.7 10.5 %copy.32 = f32[768,32,32]{0,2,1:T(8,128)} copy(f32[768,32,32]{2,1,0:T(8,128)} %fusion) | data formatting | bytes 6291456 | tf_op jit(solution)/shard_map/brl,bjl->brj/dot_general | solution.py:71
  287.2 3.5 %copy.33 = f32[768,1024]{1,0:T(8,128)} copy(f32[768,1024]{0,1:T(8,128)} %bitcast.27) | data formatting | bytes 6291456 | tf_op jit(solution)/shard_map/reshape | solution.py:72
  290.7 0.0 copy-done.1
  (10 shorter events, 0.2 us)
Async XLA Ops:
  6.5 13.1 %copy-start = (bf16[96,4096]{1,0:T(8,128)(2,1)S(1)}, bf16[96,4096]{1,0:T(8,128)(2,1)}, u32[]{:S(2)}) copy-start(bf16[96,4096]{1,0:T(8,128)(2,1)} %param.8) | copy-start | bytes 2359300
  6.5 57.5 %reduce-scatter.2.cloned.1.call-start = ((), (), s32[]{:S(2)}) async-start(), calls=%async_computation.1 | async-start | bytes 2359296 | tf_op jit(solution)/shard_map/reduce_scatter | solution.py:80
  19.4 213.9 %all-gather.3.cloned.1.call-start = ((), (), s32[]{:S(2)}) async-start(), calls=%async_computation.2 | async-start | bytes 15138816 | tf_op jit(solution)/shard_map/all_gather | solution.py:118
  113.4 18.5 %copy-start.5 = (s32[768,1]{0,1:T(1,128)S(1)}, s32[768,1]{0,1:T(1,128)}, u32[]{:S(2)}) copy-start(s32[768,1]{0,1:T(1,128)} %param.12) | copy-start | bytes 9220
  113.4 18.5 %copy-start.3 = (s32[768]{0:T(1024)S(1)}, s32[768]{0:T(1024)}, u32[]{:S(2)}) copy-start(s32[768]{0:T(1024)} %param.11) | copy-start | bytes 9220
  113.4 18.5 %copy-start.4 = (s32[768]{0:T(1024)S(1)}, s32[768]{0:T(1024)}, u32[]{:S(2)}) copy-start(s32[768]{0:T(1024)} %param.13) | copy-start | bytes 9220
  113.4 18.7 %copy-start.2 = (bf16[112,2048]{1,0:T(8,128)(2,1)S(1)}, bf16[112,2048]{1,0:T(8,128)(2,1)}, u32[]{:S(2)}) copy-start(bf16[112,2048]{1,0:T(8,128)(2,1)} %pad_maximum_fusion.1) | copy-start | bytes 1376260
  276.7 14.0 %copy-start.1 = (bf16[96,4096]{1,0:T(8,128)(2,1)S(1)}, bf16[96,4096]{1,0:T(8,128)(2,1)}, u32[]{:S(2)}) copy-start(bf16[96,4096]{1,0:T(8,128)(2,1)} %param.8) | copy-start | bytes 2359300
Sparse Core Ops, SparseCore 0:
  19.5 44.4 reduce-scatter.1
  104.8 128.4 all-gather.2

commit v2 on v1

--- a/solution.py
+++ b/solution.py
@@ -115,8 +115,18 @@
     base, node_count = level_slots(block_target)
     source_slot = base + source_offset % node_count
     source_peer = source_leaf[:, 0]
-    gathered = lax.all_gather(basis_table, "leaf", axis=0, tiled=True)
-    source_rows = gathered[source_peer * slots_per_leaf + source_slot]
+    half_slots = slots_per_leaf // 2
+    core = lax.axis_index("basis")
+    own_half = lax.dynamic_slice_in_dim(basis_table, core * half_slots, half_slots, 0)
+    gathered = lax.all_gather(own_half, "leaf", axis=0, tiled=True)
+    gathered = lax.all_gather(gathered, "basis", axis=0, tiled=True)
+    leaves = lax.axis_size("leaf")
+    source_index = (
+        (source_slot // half_slots) * (leaves * half_slots)
+        + source_peer * half_slots
+        + source_slot % half_slots
+    )
+    source_rows = gathered[source_index]
     return project(basis_table[block_target], source_rows, blocks)
 
 

time: 299 us -> 309 us (1.033)
  waiting for transfers between devices: 123 us -> 133 us
    all_gather x1 -> x2, waiting for transfers between devices: 82 us -> 91.8 us  [the longest x1 91.8 us: per_device(): gathered = lax.all_gather(own_half, 'leaf', axis=0, tiled=True)]
    unnamed x14 -> x12, local copies, waits for them, and re-layouts: 8.88 us -> 8.82 us
  transfers between devices with their start and end apart: 2 -> 3, of which waited for: 2 -> 2; matrix products, arithmetic and copies ran while one was open for 17% -> 16% of each run, Pallas kernels for 0% -> 0%
where the time goes in v2:
time: 309 us; the launch traced here: 307 us
  waiting for transfers between devices  133 us (43%)
  local copies, waits for them, and re-layouts  101 us (33%)
  blocking collectives  23 us (7%)
  matrix products  22.6 us (7%)
  between operations  13.3 us (4%)
  Pallas kernels  11.5 us (4%)
    all_gather x1, waiting for transfers between devices, per_device(): gathered = lax.all_gather(own_half, 'leaf', axis=0, tiled=True)  91.8 us
    reduce_scatter x1, waiting for transfers between devices, per_device(): lax.psum_scatter(partial_gram, ('basis', 'coup'), scatter_dimension=0, ti...  40.6 us
    all_gather x1, blocking collectives, per_device(): lax.all_gather(local_table, ('basis', 'coup'), axis=0, tiled=True)  23 us
    reshape x1, local copies, waits for them, and re-layouts, project(): coupling_mat = coupling.reshape(-1, K, K)  19.1 us
    gather x2, local copies, waits for them, and re-layouts, per_device(): source_rows = gathered[source_index]  18.8 us
    dot_general x1, matrix products, project(): jnp.einsum('brl,bjl->brj', left_prod, source_mat, preferred_element_type=...  14.3 us
    pallas_call x1, Pallas kernels, chol_basis(): pl.pallas_call(chol_kernel, out_shape=jax.ShapeDtypeStruct((count, R, K),...  11.5 us
    dot_general x1, local copies, waits for them, and re-layouts, project(): jnp.einsum('brl,bjl->brj', left_prod, source_mat, preferred_element_type=...  10.5 us
  transfers between devices with their start and end apart: 3, of which 2 were waited for; matrix products, arithmetic and copies ran while one was open for 16% of the time, Pallas kernels for 0%

profile of v2, /device:TPU:1, one launch (start us, length us, event | category | flops | bytes accessed | tf_op | source)
XLA Modules:
  0.0 307.4 jit_solution(12731136319396157624)
XLA Ops:
  6.5 0.0 copy-start
  6.5 0.0 reduce-scatter.2.cloned.1.call-start
  6.5 6.5 %reshape.44 = bf16[64,256,64]{2,1,0:T(8,128)(2,1)} reshape(bf16[64,16384]{1,0:T(8,128)(2,1)} %param.7) | data formatting | bytes 4194304 | tf_op jit(solution)/shard_map/reshape | solution.py:76
  13.1 6.3 %fusion.10 = f32[64,64,64]{2,1,0:T(8,128)} fusion(bf16[64,256,64]{2,1,0:T(8,128)(2,1)} %reshape.44), kind=kOutput, calls=%fused_computation.34 | convolution fusion | flops 134217728 | bytes 3145728 | tf_op jit(solution)/shard_map/nik,nil->nkl/dot_general | solution.py:77
  19.4 0.0 reduce-scatter.2.cloned.1.call-update
  19.4 0.2 all-gather.4.cloned.1.call-start
  19.7 0.0 copy-done
  19.7 0.1 slice.18
  19.8 0.2 slice.17
  20.0 0.8 constant_dynamic-slice_fusion.1
  20.8 0.8 constant_dynamic-slice_fusion.2
  21.6 0.8 constant_dynamic-slice_fusion.3
  22.4 0.2 reshape.56
  22.5 0.9 copy.25
  23.4 40.6 %reduce-scatter.2.cloned.1.call-done = f32[8,64,64]{2,1,0:T(8,128)} async-done(((f32[64,64,64]{2,1,0:T(8,128)}), f32[8,64,64]{2,1,0:T(8,128)}) %reduce-scatter.2.cloned.1.call-update) | async-done | bytes 131088 | tf_op jit(solution)/shard_map/reduce_scatter | solution.py:80
  64.0 1.3 fusion.11
  65.3 0.3 bitcast_reduce_fusion
  65.5 0.3 fusion.12
  65.8 0.2 bitcast_reduce_fusion.1
  66.0 1.8 pad_maximum_fusion.g_ref
  67.8 11.5 %shard_map.73 = f32[14,32,64]{2,1,0:T(8,128)} custom-call(f32[14,64,64]{2,1,0:T(8,128)} %pad_maximum_fusion.g_ref, f32[14,32,64]{2,1,0:T(8,128)} %bitcast.28), custom_call_target="tpu_custom_call" | custom-call | tf_op jit(solution)/shard_map/pallas_call | solution.py:57
  79.3 1.0 convert_element_type.12
  80.3 0.1 reshape.75
  80.4 23.0 %all-gather = bf16[8,14,2048]{2,1,0:T(8,128)(2,1)S(1)} all-gather(bf16[1,14,2048]{2,1,0:T(8,128)(2,1)S(1)} %reshape.75), channel_id=1, replica_groups=mesh['leaf'=32,'basis'=2,'coup'=4] {'basis','coup'}, dimensions={0}, use_global_device_ids=true | all-gather | bytes 516096 | tf_op jit(solution)/shard_map/all_gather | solution.py:104
  103.4 0.1 slice.28
  103.7 0.7 constant_dynamic-slice_fusion
  104.4 0.0 all-gather.4.cloned.1.call-update
  104.4 0.3 all-gather.6.cloned.1.call-start
  104.7 91.8 %all-gather.4.cloned.1.call-done = bf16[1792,2048]{1,0:T(8,128)(2,1)} async-done(((bf16[56,2048]{1,0:T(8,128)(2,1)}), bf16[1792,2048]{1,0:T(8,128)(2,1)}) %all-gather.4.cloned.1.call-update) | async-done | bytes 7340048 | tf_op jit(solution)/shard_map/all_gather | solution.py:121
  196.5 0.0 all-gather.6.cloned.1.call-update
  196.5 8.7 %copy.27 = bf16[768,4096]{0,1:T(8,128)(2,1)} copy(bf16[768,4096]{1,0:T(8,128)(2,1)} %param.10) | data formatting | bytes 12582912 | tf_op args[3]
  205.2 0.0 copy-start.4
  205.2 0.0 copy-start.2
  205.2 0.0 copy-start.3
  205.2 19.1 %copy.29 = bf16[768,64,64]{2,1,0:T(8,128)(2,1)} copy(bf16[768,64,64]{0,2,1:T(8,128)(2,1)} %bitcast.24) | data formatting | bytes 12582912 | tf_op jit(solution)/shard_map/reshape | solution.py:66
  224.2 0.0 copy-done.4
  224.3 0.0 copy-done.2
  224.3 0.0 copy-done.3
  224.3 0.1 compare_select_fusion.2
  224.5 4.2 %gather_fusion = bf16[768,2048]{1,0:T(8,128)(2,1)} fusion(bf16[112,2048]{1,0:T(8,128)(2,1)S(1)} %pad_maximum_fusion.1, s32[1024]{0:T(1024)S(1)} %pad_clamp_fusion.1), kind=kCustom, calls=%fused_computation | custom fusion | bytes 6294528 | tf_op jit(solution)/shard_map/gather | solution.py:130
  228.7 4.7 %copy.26 = bf16[768,2048]{0,1:T(8,128)(2,1)} copy(bf16[768,2048]{1,0:T(8,128)(2,1)} %gather_fusion) | data formatting | bytes 6291456 | tf_op jit(solution)/shard_map/gather | solution.py:130
  233.4 10.2 %copy.28 = bf16[768,32,64]{2,1,0:T(8,128)(2,1)} copy(bf16[768,32,64]{0,2,1:T(8,128)(2,1)} %bitcast.25) | data formatting | bytes 6291456 | tf_op jit(solution)/shard_map/reshape | solution.py:65
  243.6 0.0 all-gather.6.cloned.1.call-done
  243.6 14.1 %gather_fusion.1 = bf16[768,2048]{1,0:T(8,128)(2,1)} fusion(bf16[3584,2048]{1,0:T(8,128)(2,1)} %all-gather.6.cloned.1.call-done, s32[1024]{0:T(1024)S(1)} %pad_clamp_fusion), kind=kCustom, calls=%fused_computation.1 | custom fusion | bytes 6294528 | tf_op jit(solution)/shard_map/gather | solution.py:129
  257.7 4.7 %copy.30 = bf16[768,2048]{0,1:T(8,128)(2,1)} copy(bf16[768,2048]{1,0:T(8,128)(2,1)} %gather_fusion.1) | data formatting | bytes 6291456 | tf_op jit(solution)/shard_map/gather | solution.py:129
  262.4 10.2 %copy.31 = bf16[768,32,64]{2,1,0:T(8,128)(2,1)} copy(bf16[768,32,64]{0,2,1:T(8,128)(2,1)} %bitcast.26) | data formatting | bytes 6291456 | tf_op jit(solution)/shard_map/reshape | solution.py:70
  272.5 14.3 %fusion = f32[768,32,32]{2,1,0:T(8,128)} fusion(bf16[768,32,64]{2,1,0:T(8,128)(2,1)} %copy.31, bf16[768,32,64]{2,1,0:T(8,128)(2,1)} %copy.28, bf16[768,64,64]{2,1,0:T(8,128)(2,1)} %copy.29), kind=kOutput, calls=%fused_computation.2 | convolution fusion | flops 303562752 | bytes 15728640 | tf_op jit(solution)/shard_map/brl,bjl->brj/dot_general | solution.py:71
  286.9 0.0 copy-start.1
  286.9 10.5 %copy.32 = f32[768,32,32]{0,2,1:T(8,128)} copy(f32[768,32,32]{2,1,0:T(8,128)} %fusion) | data formatting | bytes 6291456 | tf_op jit(solution)/shard_map/brl,bjl->brj/dot_general | solution.py:71
  297.3 3.5 %copy.33 = f32[768,1024]{1,0:T(8,128)} copy(f32[768,1024]{0,1:T(8,128)} %bitcast.27) | data formatting | bytes 6291456 | tf_op jit(solution)/shard_map/reshape | solution.py:72
  300.9 0.0 copy-done.1
  (11 shorter events, 0.2 us)
Async XLA Ops:
  6.5 13.1 %copy-start = (bf16[96,4096]{1,0:T(8,128)(2,1)S(1)}, bf16[96,4096]{1,0:T(8,128)(2,1)}, u32[]{:S(2)}) copy-start(bf16[96,4096]{1,0:T(8,128)(2,1)} %param.8) | copy-start | bytes 2359300
  6.5 57.5 %reduce-scatter.2.cloned.1.call-start = ((), (), s32[]{:S(2)}) async-start(), calls=%async_computation.1 | async-start | bytes 2359296 | tf_op jit(solution)/shard_map/reduce_scatter | solution.py:80
  19.4 177.1 %all-gather.4.cloned.1.call-start = ((), (), s32[]{:S(2)}) async-start(), calls=%async_computation.2 | async-start | bytes 7569408 | tf_op jit(solution)/shard_map/all_gather | solution.py:121
  104.4 139.2 %all-gather.6.cloned.1.call-start = ((), (), s32[]{:S(2)}) async-start(), calls=%async_computation.3 | async-start | bytes 22020096 | tf_op jit(solution)/shard_map/all_gather | solution.py:122
  205.2 19.1 %copy-start.4 = (s32[768,1]{0,1:T(1,128)S(1)}, s32[768,1]{0,1:T(1,128)}, u32[]{:S(2)}) copy-start(s32[768,1]{0,1:T(1,128)} %param.12) | copy-start | bytes 9220
  205.2 19.1 %copy-start.2 = (s32[768]{0:T(1024)S(1)}, s32[768]{0:T(1024)}, u32[]{:S(2)}) copy-start(s32[768]{0:T(1024)} %param.11) | copy-start | bytes 9220
  205.2 19.1 %copy-start.3 = (s32[768]{0:T(1024)S(1)}, s32[768]{0:T(1024)}, u32[]{:S(2)}) copy-start(s32[768]{0:T(1024)} %param.13) | copy-start | bytes 9220
  286.9 14.0 %copy-start.1 = (bf16[96,4096]{1,0:T(8,128)(2,1)S(1)}, bf16[96,4096]{1,0:T(8,128)(2,1)}, u32[]{:S(2)}) copy-start(bf16[96,4096]{1,0:T(8,128)(2,1)} %param.8) | copy-start | bytes 2359300
Sparse Core Ops, SparseCore 0:
  19.5 44.4 reduce-scatter.1
  104.5 91.9 all-gather.3
  198.3 30.8 all-gather.5

commit v3 on v1

--- a/solution.py
+++ b/solution.py
@@ -61,15 +61,32 @@
     )(gram_all, sketch_t)
 
 
-def project(target_rows, source_rows, coupling):
-    target_mat = target_rows.reshape(-1, R, K)
-    coupling_mat = coupling.reshape(-1, K, K)
+def project_kernel(t_ref, s_ref, src_ref, o_ref):
+    tile = t_ref.shape[0]
+    target_mat = t_ref[...].reshape(tile, R, K)
+    coupling_mat = s_ref[...].reshape(tile, K, K)
+    source_mat = src_ref[...].reshape(tile, R, K)
     left_prod = jnp.einsum(
         "brk,bkl->brl", target_mat, coupling_mat, preferred_element_type=jnp.float32
     ).astype(jnp.bfloat16)
-    source_mat = source_rows.reshape(-1, R, K)
     result = jnp.einsum("brl,bjl->brj", left_prod, source_mat, preferred_element_type=jnp.float32)
-    return result.reshape(-1, R * R)
+    o_ref[...] = result.reshape(tile, R * R)
+
+
+def project(target_rows, source_rows, coupling):
+    count = coupling.shape[0]
+    tile = 128 if count % 128 == 0 else count
+    return pl.pallas_call(
+        project_kernel,
+        grid=(count // tile,),
+        in_specs=[
+            pl.BlockSpec((tile, R * K), lambda i: (i, 0)),
+            pl.BlockSpec((tile, K * K), lambda i: (i, 0)),
+            pl.BlockSpec((tile, R * K), lambda i: (i, 0)),
+        ],
+        out_specs=pl.BlockSpec((tile, R * R), lambda i: (i, 0)),
+        out_shape=jax.ShapeDtypeStruct((count, R * R), jnp.float32),
+    )(target_rows, coupling, source_rows)
 
 
 def per_device(basis_rows, transfer, omega, blocks, block_target, source_leaf, source_offset):

time: 299 us -> 270 us (0.903)
  local copies, waits for them, and re-layouts: 100 us -> 29.8 us
  waiting for transfers between devices: 123 us -> 164 us
  Pallas kernels: 11.5 us -> 26.8 us
  matrix products: 22.6 us -> 8.26 us
    reshape x4 -> x0, local copies, waits for them, and re-layouts: 42.5 us -> none  [the longest x1 18.5 us: project(): coupling_mat = coupling.reshape(-1, K, K)]
    all_gather x1, waiting for transfers between devices: 82 us -> 123 us  [per_device(): gathered = lax.all_gather(basis_table, 'leaf', axis=0, tiled=True)]
    pallas_call x0 -> x1, Pallas kernels: none -> 15.3 us  [project(): pl.pallas_call(project_kernel, grid=(count // tile,), in_specs=[pl.BlockS...]
    dot_general x1 -> x0, matrix products: 14.4 us -> none  [project(): jnp.einsum('brl,bjl->brj', left_prod, source_mat, preferred_element_type=...]
    dot_general x1 -> x0, local copies, waits for them, and re-layouts: 10.5 us -> none  [project(): jnp.einsum('brl,bjl->brj', left_prod, source_mat, preferred_element_type=...]
    unnamed x14 -> x11, local copies, waits for them, and re-layouts: 8.88 us -> 0.97 us
    gather x2 -> x1, local copies, waits for them, and re-layouts: 8.94 us -> 4.26 us  [per_device(): return project(basis_table[block_target], source_rows, blocks)]
    gather x2 -> x1, local copies, waits for them, and re-layouts: 18.8 us -> 14.2 us  [per_device(): source_rows = gathered[source_peer * slots_per_leaf + source_slot]]
  transfers between devices with their start and end apart: 2 -> 2, of which waited for: 2 -> 2; matrix products, arithmetic and copies ran while one was open for 17% -> 3% of each run, Pallas kernels for 0% -> 0%
where the time goes in v3:
time: 270 us
  waiting for transfers between devices  164 us (61%)
  local copies, waits for them, and re-layouts  29.8 us (11%)
  Pallas kernels  26.8 us (10%)
  blocking collectives  23.2 us (9%)
  between operations  13.6 us (5%)
  matrix products  8.26 us (3%)
  other arithmetic  3.71 us (1%)
    all_gather x1, waiting for transfers between devices, per_device(): gathered = lax.all_gather(basis_table, 'leaf', axis=0, tiled=True)  123 us
    reduce_scatter x1, waiting for transfers between devices, per_device(): lax.psum_scatter(partial_gram, ('basis', 'coup'), scatter_dimension=0, ti...  40.6 us
    all_gather x1, blocking collectives, per_device(): lax.all_gather(local_table, ('basis', 'coup'), axis=0, tiled=True)  23.2 us
    pallas_call x1, Pallas kernels, project(): pl.pallas_call(project_kernel, grid=(count // tile,), in_specs=[pl.BlockS...  15.3 us
    gather x1, local copies, waits for them, and re-layouts, per_device(): source_rows = gathered[source_peer * slots_per_leaf + source_slot]  14.2 us
    pallas_call x1, Pallas kernels, chol_basis(): pl.pallas_call(chol_kernel, out_shape=jax.ShapeDtypeStruct((count, R, K),...  11.5 us
    reshape x1, local copies, waits for them, and re-layouts, per_device(): rows_local = basis_rows.reshape(NB, -1, K)  6.54 us
    dot_general x1, matrix products, per_device(): jnp.einsum('nik,nil->nkl', rows_local, rows_local, preferred_element_type...  6.3 us
  transfers between devices with their start and end apart: 2, of which 2 were waited for; matrix products, arithmetic and copies ran while one was open for 3% of the time, Pallas kernels for 0%

profile of v3, /device:TPU:1, one launch (start us, length us, event | category | flops | bytes accessed | tf_op | source)
XLA Modules:
  0.0 269.6 jit_solution(2992501838654386618)
XLA Ops:
  6.5 0.0 copy-start
  6.5 0.0 reduce-scatter.2.cloned.1.call-start
  6.5 6.5 %reshape.32 = bf16[64,256,64]{2,1,0:T(8,128)(2,1)} reshape(bf16[64,16384]{1,0:T(8,128)(2,1)} %param.7) | data formatting | bytes 4194304 | tf_op jit(solution)/shard_map/reshape | solution.py:93
  13.1 6.3 %fusion.3 = f32[64,64,64]{2,1,0:T(8,128)} fusion(bf16[64,256,64]{2,1,0:T(8,128)(2,1)} %reshape.32), kind=kOutput, calls=%fused_computation.23 | convolution fusion | flops 134217728 | bytes 3145728 | tf_op jit(solution)/shard_map/nik,nil->nkl/dot_general | solution.py:94
  19.4 0.0 reduce-scatter.2.cloned.1.call-update
  19.4 0.2 all-gather.3.cloned.1.call-start
  19.6 0.0 copy-done
  19.7 0.1 slice.18
  19.8 0.2 slice.17
  20.0 0.8 constant_dynamic-slice_fusion
  20.8 0.8 constant_dynamic-slice_fusion.1
  21.6 0.8 constant_dynamic-slice_fusion.2
  22.4 0.2 reshape.40
  22.5 0.9 copy.19
  23.4 40.6 %reduce-scatter.2.cloned.1.call-done = f32[8,64,64]{2,1,0:T(8,128)} async-done(((f32[64,64,64]{2,1,0:T(8,128)}), f32[8,64,64]{2,1,0:T(8,128)}) %reduce-scatter.2.cloned.1.call-update) | async-done | bytes 131088 | tf_op jit(solution)/shard_map/reduce_scatter | solution.py:97
  64.0 1.3 fusion.4
  65.3 0.3 bitcast_reduce_fusion
  65.5 0.0 copy-start.4
  65.6 0.0 copy-start.2
  65.6 0.0 copy-start.3
  65.6 0.3 fusion.5
  65.8 0.2 bitcast_reduce_fusion.1
  66.0 1.8 pad_maximum_fusion.g_ref
  67.8 11.5 %shard_map.73 = f32[14,32,64]{2,1,0:T(8,128)} custom-call(f32[14,64,64]{2,1,0:T(8,128)} %pad_maximum_fusion.g_ref, f32[14,32,64]{2,1,0:T(8,128)} %bitcast.17), custom_call_target="tpu_custom_call" | custom-call | tf_op jit(solution)/shard_map/pallas_call | solution.py:57
  79.3 1.0 convert_element_type.9
  80.3 0.1 reshape.59
  80.4 23.2 %all-gather = bf16[8,14,2048]{2,1,0:T(8,128)(2,1)S(1)} all-gather(bf16[1,14,2048]{2,1,0:T(8,128)(2,1)S(1)} %reshape.59), channel_id=1, replica_groups=mesh['leaf'=32,'basis'=2,'coup'=4] {'basis','coup'}, dimensions={0}, use_global_device_ids=true | all-gather | bytes 516096 | tf_op jit(solution)/shard_map/all_gather | solution.py:121
  103.7 0.1 slice.28
  103.9 0.8 pad_maximum_fusion.1
  104.7 0.0 copy-start.1
  104.7 0.0 all-gather.3.cloned.1.call-update
  104.7 0.0 copy-done.4
  104.7 0.0 copy-done.2
  104.7 0.0 copy-done.3
  104.8 0.1 compare_select_fusion
  104.9 0.8 copy-done.1
  105.7 4.3 %gather_fusion = bf16[768,2048]{1,0:T(8,128)(2,1)} fusion(bf16[112,2048]{1,0:T(8,128)(2,1)S(1)} %copy-done.1, s32[1024]{0:T(1024)S(1)} %get-tuple-element.8), kind=kCustom, calls=%fused_computation | custom fusion | bytes 6294528 | tf_op jit(solution)/shard_map/gather | solution.py:137
  110.0 123.3 %all-gather.3.cloned.1.call-done = bf16[3584,2048]{1,0:T(8,128)(2,1)} async-done(((bf16[112,2048]{1,0:T(8,128)(2,1)}), bf16[3584,2048]{1,0:T(8,128)(2,1)}) %all-gather.3.cloned.1.call-update) | async-done | bytes 14680080 | tf_op jit(solution)/shard_map/all_gather | solution.py:135
  233.3 14.2 %gather_fusion.1 = bf16[768,2048]{1,0:T(8,128)(2,1)} fusion(bf16[3584,2048]{1,0:T(8,128)(2,1)} %all-gather.3.cloned.1.call-done, s32[1024]{0:T(1024)S(1)} %get-tuple-element.7), kind=kCustom, calls=%fused_computation.1 | custom fusion | bytes 6294528 | tf_op jit(solution)/shard_map/gather | solution.py:136
  247.5 15.3 %shard_map.74 = f32[768,1024]{1,0:T(8,128)} custom-call(bf16[768,2048]{1,0:T(8,128)(2,1)} %gather_fusion, bf16[768,4096]{1,0:T(8,128)(2,1)} %s_ref.1, bf16[768,2048]{1,0:T(8,128)(2,1)} %gather_fusion.1), custom_call_target="tpu_custom_call" | custom-call | tf_op jit(solution)/shard_map/pallas_call | solution.py:79
  (9 shorter events, 0.2 us)
Async XLA Ops:
  6.5 13.1 %copy-start = (bf16[96,4096]{1,0:T(8,128)(2,1)S(1)}, bf16[96,4096]{1,0:T(8,128)(2,1)}, u32[]{:S(2)}) copy-start(bf16[96,4096]{1,0:T(8,128)(2,1)} %param.8) | copy-start | bytes 2359300
  6.5 57.5 %reduce-scatter.2.cloned.1.call-start = ((), (), s32[]{:S(2)}) async-start(), calls=%async_computation.1 | async-start | bytes 2359296 | tf_op jit(solution)/shard_map/reduce_scatter | solution.py:97
  19.4 213.9 %all-gather.3.cloned.1.call-start = ((), (), s32[]{:S(2)}) async-start(), calls=%async_computation.2 | async-start | bytes 15138816 | tf_op jit(solution)/shard_map/all_gather | solution.py:135
  65.5 39.2 %copy-start.4 = (s32[768,1]{0,1:T(1,128)S(1)}, s32[768,1]{0,1:T(1,128)}, u32[]{:S(2)}) copy-start(s32[768,1]{0,1:T(1,128)} %param.12) | copy-start | bytes 9220
  65.6 39.2 %copy-start.2 = (s32[768]{0:T(1024)S(1)}, s32[768]{0:T(1024)}, u32[]{:S(2)}) copy-start(s32[768]{0:T(1024)} %param.13) | copy-start | bytes 9220
  65.6 39.2 %copy-start.3 = (s32[768]{0:T(1024)S(1)}, s32[768]{0:T(1024)}, u32[]{:S(2)}) copy-start(s32[768]{0:T(1024)} %param.11) | copy-start | bytes 9220
  104.7 1.0 copy-start.1
Sparse Core Ops, SparseCore 0:
  19.5 44.4 reduce-scatter.1
  104.8 128.4 all-gather.2

commit v4 on v3

--- a/solution.py
+++ b/solution.py
@@ -129,11 +129,14 @@
         axis=0,
     )
     slots_per_leaf = basis_table.shape[0]
+    local_rows = local_table.shape[0]
     base, node_count = level_slots(block_target)
-    source_slot = base + source_offset % node_count
-    source_peer = source_leaf[:, 0]
-    gathered = lax.all_gather(basis_table, "leaf", axis=0, tiled=True)
-    source_rows = gathered[source_peer * slots_per_leaf + source_slot]
+    within = source_offset % node_count
+    per_member = node_count // group
+    source_member = source_leaf[:, 0] * group + within // per_member
+    source_index = source_member * local_rows + base // group + within % per_member
+    gathered = lax.all_gather(local_table, ("leaf", "basis", "coup"), axis=0, tiled=True)
+    source_rows = gathered[source_index]
     return project(basis_table[block_target], source_rows, blocks)
 
 

time: 270 us -> 263 us (0.974)
  waiting for transfers between devices: 164 us -> 137 us
  local copies, waits for them, and re-layouts: 29.8 us -> 49.2 us
    all_gather x1, waiting for transfers between devices: 123 us -> 96.7 us  [per_device(): lax.all_gather(local_table, ('leaf', 'basis', 'coup'), axis=0, tiled=True)]
    unnamed x11 -> x10, local copies, waits for them, and re-layouts: 0.97 us -> 20.4 us
where the time goes in v4:
time: 263 us; the launch traced here: 262 us
  waiting for transfers between devices  137 us (52%)
  local copies, waits for them, and re-layouts  49.2 us (19%)
  Pallas kernels  26.8 us (10%)
  blocking collectives  23.8 us (9%)
  between operations  13.6 us (5%)
  matrix products  8.26 us (3%)
  other arithmetic  3.06 us (1%)
    all_gather x1, waiting for transfers between devices, per_device(): lax.all_gather(local_table, ('leaf', 'basis', 'coup'), axis=0, tiled=True)  96.7 us
    reduce_scatter x1, waiting for transfers between devices, per_device(): lax.psum_scatter(partial_gram, ('basis', 'coup'), scatter_dimension=0, ti...  40.5 us
    all_gather x1, blocking collectives, per_device(): lax.all_gather(local_table, ('basis', 'coup'), axis=0, tiled=True)  23.8 us
    unnamed x10, local copies, waits for them, and re-layouts  20.4 us
    pallas_call x1, Pallas kernels, project(): pl.pallas_call(project_kernel, grid=(count // tile,), in_specs=[pl.BlockS...  15.3 us
    gather x1, local copies, waits for them, and re-layouts, per_device(): source_rows = gathered[source_index]  14.2 us
    pallas_call x1, Pallas kernels, chol_basis(): pl.pallas_call(chol_kernel, out_shape=jax.ShapeDtypeStruct((count, R, K),...  11.5 us
    reshape x1, local copies, waits for them, and re-layouts, per_device(): rows_local = basis_rows.reshape(NB, -1, K)  6.55 us
  transfers between devices with their start and end apart: 2, of which 2 were waited for; matrix products, arithmetic and copies ran while one was open for 3% of the time, Pallas kernels for 0%

profile of v4, /device:TPU:1, one launch (start us, length us, event | category | flops | bytes accessed | tf_op | source)
XLA Modules:
  0.0 262.3 jit_solution(14329243691918163734)
XLA Ops:
  6.5 0.0 copy-start
  6.5 0.0 reduce-scatter.2.cloned.1.call-start
  6.5 6.5 %reshape.32 = bf16[64,256,64]{2,1,0:T(8,128)(2,1)} reshape(bf16[64,16384]{1,0:T(8,128)(2,1)} %param.7) | data formatting | bytes 4194304 | tf_op jit(solution)/shard_map/reshape | solution.py:93
  13.1 6.3 %fusion.10 = f32[64,64,64]{2,1,0:T(8,128)} fusion(bf16[64,256,64]{2,1,0:T(8,128)(2,1)} %reshape.32), kind=kOutput, calls=%fused_computation.44 | convolution fusion | flops 134217728 | bytes 3145728 | tf_op jit(solution)/shard_map/nik,nil->nkl/dot_general | solution.py:94
  19.4 0.0 reduce-scatter.2.cloned.1.call-update
  19.4 0.2 all-gather.4.cloned.1.call-start
  19.7 0.0 copy-done
  19.7 0.0 copy-start.3
  19.7 0.0 copy-start.1
  19.7 0.0 copy-start.2
  19.7 0.2 slice.17
  19.9 0.1 slice.18
  20.1 0.8 constant_dynamic-slice_fusion
  20.8 0.8 constant_dynamic-slice_fusion.1
  21.6 0.8 constant_dynamic-slice_fusion.2
  22.4 0.2 reshape.40
  22.6 0.9 copy.19
  23.4 40.5 %reduce-scatter.2.cloned.1.call-done = f32[8,64,64]{2,1,0:T(8,128)} async-done(((f32[64,64,64]{2,1,0:T(8,128)}), f32[8,64,64]{2,1,0:T(8,128)}) %reduce-scatter.2.cloned.1.call-update) | async-done | bytes 131088 | tf_op jit(solution)/shard_map/reduce_scatter | solution.py:97
  64.0 1.3 fusion.11
  65.2 0.3 bitcast_reduce_fusion
  65.5 0.3 fusion.12
  65.8 0.2 bitcast_reduce_fusion.1
  66.0 1.8 pad_maximum_fusion.g_ref
  67.7 11.5 %shard_map.73 = f32[14,32,64]{2,1,0:T(8,128)} custom-call(f32[14,64,64]{2,1,0:T(8,128)} %pad_maximum_fusion.g_ref, f32[14,32,64]{2,1,0:T(8,128)} %bitcast.17), custom_call_target="tpu_custom_call" | custom-call | tf_op jit(solution)/shard_map/pallas_call | solution.py:57
  79.2 1.0 convert_element_type.9
  80.2 0.8 reshape.59
  81.0 0.0 all-gather.4.cloned.1.call-update
  81.0 0.0 copy-done.3
  81.0 0.0 copy-done.1
  81.0 0.0 copy-done.2
  81.1 0.3 compare_select_fusion
  81.3 23.8 %all-gather = bf16[8,14,2048]{2,1,0:T(8,128)(2,1)S(1)} all-gather(bf16[1,14,2048]{2,1,0:T(8,128)(2,1)} %reshape.59), channel_id=1, replica_groups=mesh['leaf'=32,'basis'=2,'coup'=4] {'basis','coup'}, dimensions={0}, use_global_device_ids=true | all-gather | bytes 516096 | tf_op jit(solution)/shard_map/all_gather | solution.py:121
  105.2 0.1 slice.28
  105.4 4.3 %gather_fusion = bf16[768,2048]{1,0:T(8,128)(2,1)} fusion(bf16[112,2048]{1,0:T(8,128)(2,1)S(1)} %pad_maximum_fusion.1, s32[1024]{0:T(1024)S(1)} %get-tuple-element.8), kind=kCustom, calls=%fused_computation | custom fusion | bytes 6294528 | tf_op jit(solution)/shard_map/gather | solution.py:140
  109.7 96.7 %all-gather.4.cloned.1.call-done = bf16[256,14,2048]{2,1,0:T(8,128)(2,1)} async-done(((bf16[1,14,2048]{2,1,0:T(8,128)(2,1)}), bf16[256,14,2048]{2,1,0:T(8,128)(2,1)}) %all-gather.4.cloned.1.call-update) | async-done | bytes 14680080 | tf_op jit(solution)/shard_map/all_gather | solution.py:138
  206.4 19.6 %reshape.62 = bf16[3584,2048]{1,0:T(8,128)(2,1)} reshape(bf16[256,14,2048]{2,1,0:T(8,128)(2,1)} %all-gather.4.cloned.1.call-done) | data formatting | bytes 29360128
  226.0 14.2 %gather_fusion.1 = bf16[768,2048]{1,0:T(8,128)(2,1)} fusion(bf16[3584,2048]{1,0:T(8,128)(2,1)} %reshape.62, s32[1024]{0:T(1024)S(1)} %get-tuple-element.7), kind=kCustom, calls=%fused_computation.1 | custom fusion | bytes 6294528 | tf_op jit(solution)/shard_map/gather | solution.py:139
  240.2 15.3 %shard_map.74 = f32[768,1024]{1,0:T(8,128)} custom-call(bf16[768,2048]{1,0:T(8,128)(2,1)} %gather_fusion, bf16[768,4096]{1,0:T(8,128)(2,1)} %s_ref.1, bf16[768,2048]{1,0:T(8,128)(2,1)} %gather_fusion.1), custom_call_target="tpu_custom_call" | custom-call | tf_op jit(solution)/shard_map/pallas_call | solution.py:79
  (10 shorter events, 0.2 us)
Async XLA Ops:
  6.5 13.1 %copy-start = (bf16[96,4096]{1,0:T(8,128)(2,1)S(1)}, bf16[96,4096]{1,0:T(8,128)(2,1)}, u32[]{:S(2)}) copy-start(bf16[96,4096]{1,0:T(8,128)(2,1)} %param.8) | copy-start | bytes 2359300
  6.5 57.4 %reduce-scatter.2.cloned.1.call-start = ((), (), s32[]{:S(2)}) async-start(), calls=%async_computation.1 | async-start | bytes 2359296 | tf_op jit(solution)/shard_map/reduce_scatter | solution.py:97
  19.4 187.0 %all-gather.4.cloned.1.call-start = ((), (), s32[]{:S(2)}) async-start(), calls=%async_computation.2 | async-start | bytes 16842752 | tf_op jit(solution)/shard_map/all_gather | solution.py:138
  19.7 61.3 %copy-start.3 = (s32[768,1]{0,1:T(1,128)S(1)}, s32[768,1]{0,1:T(1,128)}, u32[]{:S(2)}) copy-start(s32[768,1]{0,1:T(1,128)} %param.12) | copy-start | bytes 9220
  19.7 61.4 %copy-start.1 = (s32[768]{0:T(1024)S(1)}, s32[768]{0:T(1024)}, u32[]{:S(2)}) copy-start(s32[768]{0:T(1024)} %param.13) | copy-start | bytes 9220
  19.7 61.4 %copy-start.2 = (s32[768]{0:T(1024)S(1)}, s32[768]{0:T(1024)}, u32[]{:S(2)}) copy-start(s32[768]{0:T(1024)} %param.11) | copy-start | bytes 9220
Sparse Core Ops, SparseCore 0:
  19.5 44.3 reduce-scatter.1
  81.1 125.2 all-gather.3

commit v5 on v4

--- a/solution.py
+++ b/solution.py
@@ -61,32 +61,42 @@
     )(gram_all, sketch_t)
 
 
-def project_kernel(t_ref, s_ref, src_ref, o_ref):
+def left_kernel(t_ref, s_ref, o_ref):
     tile = t_ref.shape[0]
     target_mat = t_ref[...].reshape(tile, R, K)
     coupling_mat = s_ref[...].reshape(tile, K, K)
-    source_mat = src_ref[...].reshape(tile, R, K)
     left_prod = jnp.einsum(
         "brk,bkl->brl", target_mat, coupling_mat, preferred_element_type=jnp.float32
-    ).astype(jnp.bfloat16)
+    )
+    o_ref[...] = left_prod.astype(jnp.bfloat16).reshape(tile, R * K)
+
+
+def right_kernel(l_ref, src_ref, o_ref):
+    tile = l_ref.shape[0]
+    left_prod = l_ref[...].reshape(tile, R, K)
+    source_mat = src_ref[...].reshape(tile, R, K)
     result = jnp.einsum("brl,bjl->brj", left_prod, source_mat, preferred_element_type=jnp.float32)
     o_ref[...] = result.reshape(tile, R * R)
 
 
-def project(target_rows, source_rows, coupling):
-    count = coupling.shape[0]
+def row_tiled(kernel, widths, out_width, out_dtype, *arrays):
+    count = arrays[0].shape[0]
     tile = 128 if count % 128 == 0 else count
     return pl.pallas_call(
-        project_kernel,
+        kernel,
         grid=(count // tile,),
-        in_specs=[
-            pl.BlockSpec((tile, R * K), lambda i: (i, 0)),
-            pl.BlockSpec((tile, K * K), lambda i: (i, 0)),
-            pl.BlockSpec((tile, R * K), lambda i: (i, 0)),
-        ],
-        out_specs=pl.BlockSpec((tile, R * R), lambda i: (i, 0)),
-        out_shape=jax.ShapeDtypeStruct((count, R * R), jnp.float32),
-    )(target_rows, coupling, source_rows)
+        in_specs=[pl.BlockSpec((tile, w), lambda i: (i, 0)) for w in widths],
+        out_specs=pl.BlockSpec((tile, out_width), lambda i: (i, 0)),
+        out_shape=jax.ShapeDtypeStruct((count, out_width), out_dtype),
+    )(*arrays)
+
+
+def left_product(target_rows, coupling):
+    return row_tiled(left_kernel, (R * K, K * K), R * K, jnp.bfloat16, target_rows, coupling)
+
+
+def right_product(left_rows, source_rows):
+    return row_tiled(right_kernel, (R * K, R * K), R * R, jnp.float32, left_rows, source_rows)
 
 
 def per_device(basis_rows, transfer, omega, blocks, block_target, source_leaf, source_offset):
@@ -129,15 +139,17 @@
         axis=0,
     )
     slots_per_leaf = basis_table.shape[0]
-    local_rows = local_table.shape[0]
+    left_rows = left_product(basis_table[block_target], blocks)
+    local_rows = -(-local_table.shape[0] // 8) * 8
+    padded_table = jnp.pad(local_table, ((0, local_rows - local_table.shape[0]), (0, 0)))
     base, node_count = level_slots(block_target)
     within = source_offset % node_count
     per_member = node_count // group
     source_member = source_leaf[:, 0] * group + within // per_member
     source_index = source_member * local_rows + base // group + within % per_member
-    gathered = lax.all_gather(local_table, ("leaf", "basis", "coup"), axis=0, tiled=True)
+    gathered = lax.all_gather(padded_table, ("leaf", "basis", "coup"), axis=0, tiled=True)
     source_rows = gathered[source_index]
-    return project(basis_table[block_target], source_rows, blocks)
+    return right_product(left_rows, source_rows)
 
 
 def solution(mesh):

time: 263 us -> 239 us (0.909)
  local copies, waits for them, and re-layouts: 49.2 us -> 30.6 us
  waiting for transfers between devices: 137 us -> 126 us
  Pallas kernels: 26.8 us -> 33.3 us
    unnamed x10 -> x9, local copies, waits for them, and re-layouts: 20.4 us -> 0.17 us
    all_gather x1, waiting for transfers between devices: 96.7 us -> 85.1 us  [per_device(): lax.all_gather(padded_table, ('leaf', 'basis', 'coup'), axis=0, tiled=True)]
    pallas_call x1 -> x2, Pallas kernels: 15.3 us -> 21.8 us  [row_tiled(): pl.pallas_call(kernel, grid=(count // tile,), in_specs=[pl.BlockSpec((til...]
  transfers between devices with their start and end apart: 2 -> 2, of which waited for: 2 -> 2; matrix products, arithmetic and copies ran while one was open for 3% -> 4% of each run, Pallas kernels for 0% -> 5%
where the time goes in v5:
time: 239 us; the launch traced here: 238 us
  waiting for transfers between devices  126 us (53%)
  Pallas kernels  33.3 us (14%)
  local copies, waits for them, and re-layouts  30.6 us (13%)
  blocking collectives  23.6 us (10%)
  between operations  13.6 us (6%)
  matrix products  8.26 us (3%)
  other arithmetic  3.07 us (1%)
    all_gather x1, waiting for transfers between devices, per_device(): lax.all_gather(padded_table, ('leaf', 'basis', 'coup'), axis=0, tiled=True)  85.1 us
    reduce_scatter x1, waiting for transfers between devices, per_device(): lax.psum_scatter(partial_gram, ('basis', 'coup'), scatter_dimension=0, ti...  40.5 us
    all_gather x1, blocking collectives, per_device(): lax.all_gather(local_table, ('basis', 'coup'), axis=0, tiled=True)  23.6 us
    pallas_call x2, Pallas kernels, row_tiled(): pl.pallas_call(kernel, grid=(count // tile,), in_specs=[pl.BlockSpec((til...  21.8 us
    gather x1, local copies, waits for them, and re-layouts, per_device(): source_rows = gathered[source_index]  15.1 us
    pallas_call x1, Pallas kernels, chol_basis(): pl.pallas_call(chol_kernel, out_shape=jax.ShapeDtypeStruct((count, R, K),...  11.5 us
    reshape x1, local copies, waits for them, and re-layouts, per_device(): rows_local = basis_rows.reshape(NB, -1, K)  6.54 us
    dot_general x1, matrix products, per_device(): jnp.einsum('nik,nil->nkl', rows_local, rows_local, preferred_element_type...  6.3 us
  transfers between devices with their start and end apart: 2, of which 2 were waited for; matrix products, arithmetic and copies ran while one was open for 4% of the time, Pallas kernels for 5%

profile of v5, /device:TPU:1, one launch (start us, length us, event | category | flops | bytes accessed | tf_op | source)
XLA Modules:
  0.0 238.5 jit_solution(5266949413646797516)
XLA Ops:
  6.5 0.0 copy-start
  6.5 0.0 reduce-scatter.2.cloned.1.call-start
  6.5 6.5 %reshape.32 = bf16[64,256,64]{2,1,0:T(8,128)(2,1)} reshape(bf16[64,16384]{1,0:T(8,128)(2,1)} %param.7) | data formatting | bytes 4194304 | tf_op jit(solution)/shard_map/reshape | solution.py:103
  13.1 6.3 %fusion.10 = f32[64,64,64]{2,1,0:T(8,128)} fusion(bf16[64,256,64]{2,1,0:T(8,128)(2,1)} %reshape.32), kind=kOutput, calls=%fused_computation.44 | convolution fusion | flops 134217728 | bytes 3145728 | tf_op jit(solution)/shard_map/nik,nil->nkl/dot_general | solution.py:104
  19.4 0.0 reduce-scatter.2.cloned.1.call-update
  19.4 0.2 all-gather.3.cloned.1.call-start
  19.6 0.0 copy-done
  19.7 0.1 slice.18
  19.8 0.0 copy-start.3
  19.8 0.0 copy-start.1
  19.8 0.0 copy-start.2
  19.9 0.2 slice.17
  20.1 0.8 constant_dynamic-slice_fusion
  20.8 0.8 constant_dynamic-slice_fusion.1
  21.6 0.8 constant_dynamic-slice_fusion.2
  22.4 0.2 reshape.40
  22.6 0.9 copy.19
  23.4 40.5 %reduce-scatter.2.cloned.1.call-done = f32[8,64,64]{2,1,0:T(8,128)} async-done(((f32[64,64,64]{2,1,0:T(8,128)}), f32[8,64,64]{2,1,0:T(8,128)}) %reduce-scatter.2.cloned.1.call-update) | async-done | bytes 131088 | tf_op jit(solution)/shard_map/reduce_scatter | solution.py:107
  64.0 1.3 fusion.11
  65.2 0.3 bitcast_reduce_fusion
  65.5 0.3 fusion.12
  65.8 0.2 bitcast_reduce_fusion.1
  66.0 1.8 pad_maximum_fusion.g_ref
  67.7 11.5 %shard_map.73 = f32[14,32,64]{2,1,0:T(8,128)} custom-call(f32[14,64,64]{2,1,0:T(8,128)} %pad_maximum_fusion.g_ref, f32[14,32,64]{2,1,0:T(8,128)} %bitcast.17), custom_call_target="tpu_custom_call" | custom-call | tf_op jit(solution)/shard_map/pallas_call | solution.py:57
  79.2 1.0 convert_element_type.11
  80.2 0.1 reshape.35
  80.3 0.6 pad.4
  81.0 0.0 all-gather.3.cloned.1.call-update
  81.0 0.0 copy-done.3
  81.0 0.0 copy-done.1
  81.0 0.0 copy-done.2
  81.0 0.3 compare_select_fusion
  81.3 0.1 reshape.59
  81.5 23.6 %all-gather = bf16[8,14,2048]{2,1,0:T(8,128)(2,1)S(1)} all-gather(bf16[1,14,2048]{2,1,0:T(8,128)(2,1)S(1)} %reshape.59), channel_id=1, replica_groups=mesh['leaf'=32,'basis'=2,'coup'=4] {'basis','coup'}, dimensions={0}, use_global_device_ids=true | all-gather | bytes 516096 | tf_op jit(solution)/shard_map/all_gather | solution.py:131
  105.1 0.1 slice.28
  105.4 4.2 %gather_fusion = bf16[768,2048]{1,0:T(8,128)(2,1)} fusion(bf16[112,2048]{1,0:T(8,128)(2,1)S(1)} %pad_maximum_fusion.1, s32[1024]{0:T(1024)S(1)} %pad_clamp_fusion.1), kind=kCustom, calls=%fused_computation | custom fusion | bytes 6294528 | tf_op jit(solution)/shard_map/gather | solution.py:142
  109.6 11.7 %shard_map.74.l_ref = bf16[768,2048]{1,0:T(8,128)(2,1)} custom-call(bf16[768,2048]{1,0:T(8,128)(2,1)} %gather_fusion, bf16[768,4096]{1,0:T(8,128)(2,1)} %s_ref.1), custom_call_target="tpu_custom_call" | custom-call | tf_op jit(solution)/shard_map/pallas_call | solution.py:85
  121.3 85.1 %all-gather.3.cloned.1.call-done = bf16[4096,2048]{1,0:T(8,128)(2,1)} async-done(((bf16[16,2048]{1,0:T(8,128)(2,1)}), bf16[4096,2048]{1,0:T(8,128)(2,1)}) %all-gather.3.cloned.1.call-update) | async-done | bytes 16777232 | tf_op jit(solution)/shard_map/all_gather | solution.py:150
  206.4 15.1 %gather_fusion.1 = bf16[768,2048]{1,0:T(8,128)(2,1)} fusion(bf16[4096,2048]{1,0:T(8,128)(2,1)} %all-gather.3.cloned.1.call-done, s32[1024]{0:T(1024)S(1)} %pad_clamp_fusion), kind=kCustom, calls=%fused_computation.1 | custom fusion | bytes 6294528 | tf_op jit(solution)/shard_map/gather | solution.py:151
  221.4 10.2 %shard_map.75 = f32[768,1024]{1,0:T(8,128)} custom-call(bf16[768,2048]{1,0:T(8,128)(2,1)} %shard_map.74.l_ref, bf16[768,2048]{1,0:T(8,128)(2,1)} %gather_fusion.1), custom_call_target="tpu_custom_call" | custom-call | tf_op jit(solution)/shard_map/pallas_call | solution.py:85
  (11 shorter events, 0.2 us)
Async XLA Ops:
  6.5 13.1 %copy-start = (bf16[96,4096]{1,0:T(8,128)(2,1)S(1)}, bf16[96,4096]{1,0:T(8,128)(2,1)}, u32[]{:S(2)}) copy-start(bf16[96,4096]{1,0:T(8,128)(2,1)} %param.8) | copy-start | bytes 2359300
  6.5 57.4 %reduce-scatter.2.cloned.1.call-start = ((), (), s32[]{:S(2)}) async-start(), calls=%async_computation.1 | async-start | bytes 2359296 | tf_op jit(solution)/shard_map/reduce_scatter | solution.py:107
  19.4 187.0 %all-gather.3.cloned.1.call-start = ((), (), s32[]{:S(2)}) async-start(), calls=%async_computation.2 | async-start | bytes 16842752 | tf_op jit(solution)/shard_map/all_gather | solution.py:150
  19.8 61.2 %copy-start.3 = (s32[768,1]{0,1:T(1,128)S(1)}, s32[768,1]{0,1:T(1,128)}, u32[]{:S(2)}) copy-start(s32[768,1]{0,1:T(1,128)} %param.12) | copy-start | bytes 9220
  19.8 61.2 %copy-start.1 = (s32[768]{0:T(1024)S(1)}, s32[768]{0:T(1024)}, u32[]{:S(2)}) copy-start(s32[768]{0:T(1024)} %param.13) | copy-start | bytes 9220
  19.8 61.2 %copy-start.2 = (s32[768]{0:T(1024)S(1)}, s32[768]{0:T(1024)}, u32[]{:S(2)}) copy-start(s32[768]{0:T(1024)} %param.11) | copy-start | bytes 9220
Sparse Core Ops, SparseCore 0:
  19.5 44.3 reduce-scatter.1
  81.1 125.2 all-gather.2

commit v6 on v5

--- a/solution.py
+++ b/solution.py
@@ -99,11 +99,26 @@
     return row_tiled(right_kernel, (R * K, R * K), R * R, jnp.float32, left_rows, source_rows)
 
 
+def gram_kernel(x_ref, o_ref):
+    tile = x_ref.shape[0]
+    rows = x_ref[...].reshape(tile, -1, K)
+    o_ref[...] = jnp.einsum("nik,nil->nkl", rows, rows, preferred_element_type=jnp.float32)
+
+
+def local_gram(basis_rows):
+    count, width = basis_rows.shape
+    tile = 32 if count % 32 == 0 else count
+    return pl.pallas_call(
+        gram_kernel,
+        grid=(count // tile,),
+        in_specs=[pl.BlockSpec((tile, width), lambda i: (i, 0))],
+        out_specs=pl.BlockSpec((tile, K, K), lambda i: (i, 0, 0)),
+        out_shape=jax.ShapeDtypeStruct((count, K, K), jnp.float32),
+    )(basis_rows)
+
+
 def per_device(basis_rows, transfer, omega, blocks, block_target, source_leaf, source_offset):
-    rows_local = basis_rows.reshape(NB, -1, K)
-    partial_gram = jnp.einsum(
-        "nik,nil->nkl", rows_local, rows_local, preferred_element_type=jnp.float32
-    )
+    partial_gram = local_gram(basis_rows)
     gram_share = lax.psum_scatter(partial_gram, ("basis", "coup"), scatter_dimension=0, tiled=True)
     group = lax.axis_size(("basis", "coup"))
     member = lax.axis_index(("basis", "coup"))

time: 239 us -> 231 us (0.967)
  local copies, waits for them, and re-layouts: 30.6 us -> 24.1 us
  matrix products: 8.26 us -> 1.95 us
  Pallas kernels: 33.3 us -> 38 us
    reshape x1 -> x0, local copies, waits for them, and re-layouts: 6.54 us -> none  [per_device(): rows_local = basis_rows.reshape(NB, -1, K)]
    dot_general x1 -> x0, matrix products: 6.3 us -> none  [per_device(): jnp.einsum('nik,nil->nkl', rows_local, rows_local, preferred_element_type...]
    pallas_call x0 -> x1, Pallas kernels: none -> 4.61 us  [local_gram(): pl.pallas_call(gram_kernel, grid=(count // tile,), in_specs=[pl.BlockSpec...]
where the time goes in v6:
time: 231 us; the launch traced here: 230 us
  waiting for transfers between devices  126 us (55%)
  Pallas kernels  38 us (16%)
  local copies, waits for them, and re-layouts  24.1 us (10%)
  blocking collectives  23.6 us (10%)
  between operations  13.6 us (6%)
  other arithmetic  3.07 us (1%)
    all_gather x1, waiting for transfers between devices, per_device(): lax.all_gather(padded_table, ('leaf', 'basis', 'coup'), axis=0, tiled=True)  85.2 us
    reduce_scatter x1, waiting for transfers between devices, per_device(): lax.psum_scatter(partial_gram, ('basis', 'coup'), scatter_dimension=0, ti...  40.7 us
    all_gather x1, blocking collectives, per_device(): lax.all_gather(local_table, ('basis', 'coup'), axis=0, tiled=True)  23.6 us
    pallas_call x2, Pallas kernels, row_tiled(): pl.pallas_call(kernel, grid=(count // tile,), in_specs=[pl.BlockSpec((til...  21.8 us
    gather x1, local copies, waits for them, and re-layouts, per_device(): source_rows = gathered[source_index]  15.1 us
    pallas_call x1, Pallas kernels, chol_basis(): pl.pallas_call(chol_kernel, out_shape=jax.ShapeDtypeStruct((count, R, K),...  11.5 us
  transfers between devices with their start and end apart: 2, of which 2 were waited for; matrix products, arithmetic and copies ran while one was open for 4% of the time, Pallas kernels for 5%

profile of v6, /device:TPU:1, one launch (start us, length us, event | category | flops | bytes accessed | tf_op | source)
XLA Modules:
  0.0 230.3 jit_solution(16156803118844976854)
XLA Ops:
  6.5 0.0 copy-start
  6.5 0.0 reduce-scatter.2.cloned.1.call-start
  6.5 4.6 %shard_map.73 = f32[64,64,64]{2,1,0:T(8,128)} custom-call(bf16[64,16384]{1,0:T(8,128)(2,1)} %x_ref.1), custom_call_target="tpu_custom_call" | custom-call | tf_op jit(solution)/shard_map/pallas_call | solution.py:111
  11.2 0.0 reduce-scatter.2.cloned.1.call-update
  11.2 0.0 all-gather.3.cloned.1.call-start
  11.2 0.0 copy-done
  11.3 0.1 slice.18
  11.4 0.0 copy-start.3
  11.4 0.0 copy-start.1
  11.4 0.0 copy-start.2
  11.5 0.2 slice.17
  11.6 0.8 constant_dynamic-slice_fusion
  12.4 0.8 constant_dynamic-slice_fusion.1
  13.2 0.8 constant_dynamic-slice_fusion.2
  14.0 0.2 reshape.36
  14.1 0.9 copy.16
  15.0 40.7 %reduce-scatter.2.cloned.1.call-done = f32[8,64,64]{2,1,0:T(8,128)} async-done(((f32[64,64,64]{2,1,0:T(8,128)}), f32[8,64,64]{2,1,0:T(8,128)}) %reduce-scatter.2.cloned.1.call-update) | async-done | bytes 131088 | tf_op jit(solution)/shard_map/reduce_scatter | solution.py:122
  55.7 1.3 fusion.10
  57.0 0.3 bitcast_reduce_fusion
  57.3 0.3 fusion.11
  57.5 0.2 bitcast_reduce_fusion.1
  57.7 1.8 pad_maximum_fusion.g_ref
  59.5 11.5 %shard_map.74 = f32[14,32,64]{2,1,0:T(8,128)} custom-call(f32[14,64,64]{2,1,0:T(8,128)} %pad_maximum_fusion.g_ref, f32[14,32,64]{2,1,0:T(8,128)} %bitcast.15), custom_call_target="tpu_custom_call" | custom-call | tf_op jit(solution)/shard_map/pallas_call | solution.py:57
  71.0 1.0 convert_element_type.11
  72.0 0.1 reshape.31
  72.1 0.6 pad.4
  72.7 0.0 all-gather.3.cloned.1.call-update
  72.8 0.0 copy-done.3
  72.8 0.0 copy-done.1
  72.8 0.0 copy-done.2
  72.8 0.3 compare_select_fusion
  73.1 0.1 reshape.55
  73.2 23.6 %all-gather = bf16[8,14,2048]{2,1,0:T(8,128)(2,1)S(1)} all-gather(bf16[1,14,2048]{2,1,0:T(8,128)(2,1)S(1)} %reshape.55), channel_id=1, replica_groups=mesh['leaf'=32,'basis'=2,'coup'=4] {'basis','coup'}, dimensions={0}, use_global_device_ids=true | all-gather | bytes 516096 | tf_op jit(solution)/shard_map/all_gather | solution.py:146
  96.8 0.1 slice.28
  97.1 4.2 %gather_fusion = bf16[768,2048]{1,0:T(8,128)(2,1)} fusion(bf16[112,2048]{1,0:T(8,128)(2,1)S(1)} %pad_maximum_fusion.1, s32[1024]{0:T(1024)S(1)} %pad_clamp_fusion.1), kind=kCustom, calls=%fused_computation | custom fusion | bytes 6294528 | tf_op jit(solution)/shard_map/gather | solution.py:157
  101.3 11.7 %shard_map.75.l_ref = bf16[768,2048]{1,0:T(8,128)(2,1)} custom-call(bf16[768,2048]{1,0:T(8,128)(2,1)} %gather_fusion, bf16[768,4096]{1,0:T(8,128)(2,1)} %s_ref.1), custom_call_target="tpu_custom_call" | custom-call | tf_op jit(solution)/shard_map/pallas_call | solution.py:85
  113.0 85.2 %all-gather.3.cloned.1.call-done = bf16[4096,2048]{1,0:T(8,128)(2,1)} async-done(((bf16[16,2048]{1,0:T(8,128)(2,1)}), bf16[4096,2048]{1,0:T(8,128)(2,1)}) %all-gather.3.cloned.1.call-update) | async-done | bytes 16777232 | tf_op jit(solution)/shard_map/all_gather | solution.py:165
  198.2 15.1 %gather_fusion.1 = bf16[768,2048]{1,0:T(8,128)(2,1)} fusion(bf16[4096,2048]{1,0:T(8,128)(2,1)} %all-gather.3.cloned.1.call-done, s32[1024]{0:T(1024)S(1)} %pad_clamp_fusion), kind=kCustom, calls=%fused_computation.1 | custom fusion | bytes 6294528 | tf_op jit(solution)/shard_map/gather | solution.py:166
  213.3 10.2 %shard_map.76 = f32[768,1024]{1,0:T(8,128)} custom-call(bf16[768,2048]{1,0:T(8,128)(2,1)} %shard_map.75.l_ref, bf16[768,2048]{1,0:T(8,128)(2,1)} %gather_fusion.1), custom_call_target="tpu_custom_call" | custom-call | tf_op jit(solution)/shard_map/pallas_call | solution.py:85
  (11 shorter events, 0.2 us)
Async XLA Ops:
  6.5 4.7 %copy-start = (bf16[96,4096]{1,0:T(8,128)(2,1)S(1)}, bf16[96,4096]{1,0:T(8,128)(2,1)}, u32[]{:S(2)}) copy-start(bf16[96,4096]{1,0:T(8,128)(2,1)} %param.8) | copy-start | bytes 2359300
  6.5 49.2 %reduce-scatter.2.cloned.1.call-start = ((), (), s32[]{:S(2)}) async-start(), calls=%async_computation.1 | async-start | bytes 2359296 | tf_op jit(solution)/shard_map/reduce_scatter | solution.py:122
  11.2 187.0 %all-gather.3.cloned.1.call-start = ((), (), s32[]{:S(2)}) async-start(), calls=%async_computation.2 | async-start | bytes 16842752 | tf_op jit(solution)/shard_map/all_gather | solution.py:165
  11.4 61.4 %copy-start.3 = (s32[768,1]{0,1:T(1,128)S(1)}, s32[768,1]{0,1:T(1,128)}, u32[]{:S(2)}) copy-start(s32[768,1]{0,1:T(1,128)} %param.12) | copy-start | bytes 9220
  11.4 61.4 %copy-start.1 = (s32[768]{0:T(1024)S(1)}, s32[768]{0:T(1024)}, u32[]{:S(2)}) copy-start(s32[768]{0:T(1024)} %param.13) | copy-start | bytes 9220
  11.4 61.4 %copy-start.2 = (s32[768]{0:T(1024)S(1)}, s32[768]{0:T(1024)}, u32[]{:S(2)}) copy-start(s32[768]{0:T(1024)} %param.11) | copy-start | bytes 9220
Sparse Core Ops, SparseCore 0:
  11.3 44.3 reduce-scatter.1
  72.9 125.2 all-gather.2

commit v7 on v6

--- a/solution.py
+++ b/solution.py
@@ -117,9 +117,22 @@
     )(basis_rows)
 
 
+def halving_scatter(x):
+    coup_size = lax.axis_size("coup")
+    steps = [("basis", 1)] + [("coup", bit) for bit in (2, 1) if bit < coup_size]
+    for axis, bit in steps:
+        size = lax.axis_size(axis)
+        mine = (lax.axis_index(axis) // bit) % 2
+        half = x.shape[0] // 2
+        keep = lax.dynamic_slice_in_dim(x, mine * half, half, 0)
+        send = lax.dynamic_slice_in_dim(x, (1 - mine) * half, half, 0)
+        x = keep + lax.ppermute(send, axis, [(i, i ^ bit) for i in range(size)])
+    return x
+
+
 def per_device(basis_rows, transfer, omega, blocks, block_target, source_leaf, source_offset):
     partial_gram = local_gram(basis_rows)
-    gram_share = lax.psum_scatter(partial_gram, ("basis", "coup"), scatter_dimension=0, tiled=True)
+    gram_share = halving_scatter(partial_gram)
     group = lax.axis_size(("basis", "coup"))
     member = lax.axis_index(("basis", "coup"))
     local_count = NB // group

time: 231 us -> 221 us (0.957)
  waiting for transfers between devices: 126 us -> 106 us
  starting transfers between devices: 0.04 us -> 4.77 us
  local copies, waits for them, and re-layouts: 24.1 us -> 27.6 us
    reduce_scatter x1 -> x0, waiting for transfers between devices: 40.7 us -> none  [per_device(): lax.psum_scatter(partial_gram, ('basis', 'coup'), scatter_dimension=0, ti...]
    ppermute x0 -> x3, waiting for transfers between devices: none -> 18.8 us  [halving_scatter(): x = keep + lax.ppermute(send, axis, [(i, i ^ bit) for i in range(size)])]
    ppermute x0 -> x3, starting transfers between devices: none -> 4.77 us  [halving_scatter(): x = keep + lax.ppermute(send, axis, [(i, i ^ bit) for i in range(size)])]
    dynamic_slice x0 -> x3, local copies, waits for them, and re-layouts: none -> 2.52 us  [halving_scatter(): send = lax.dynamic_slice_in_dim(x, (1 - mine) * half, half, 0)]
    add x0 -> x3, other arithmetic: none -> 2.49 us  [halving_scatter(): x = keep + lax.ppermute(send, axis, [(i, i ^ bit) for i in range(size)])]
  transfers between devices with their start and end apart: 2 -> 4, of which waited for: 2 -> 4; matrix products, arithmetic and copies ran while one was open for 4% -> 4% of each run, Pallas kernels for 5% -> 5%
where the time goes in v7:
time: 221 us; the launch traced here: 220 us
  waiting for transfers between devices  106 us (48%)
  Pallas kernels  38 us (17%)
  local copies, waits for them, and re-layouts  27.6 us (12%)
  blocking collectives  24.6 us (11%)
  between operations  13.7 us (6%)
  starting transfers between devices  4.77 us (2%)
  other arithmetic  4.59 us (2%)
    all_gather x1, waiting for transfers between devices, per_device(): lax.all_gather(padded_table, ('leaf', 'basis', 'coup'), axis=0, tiled=True)  87.2 us
    all_gather x1, blocking collectives, per_device(): lax.all_gather(local_table, ('basis', 'coup'), axis=0, tiled=True)  24.6 us
    pallas_call x2, Pallas kernels, row_tiled(): pl.pallas_call(kernel, grid=(count // tile,), in_specs=[pl.BlockSpec((til...  21.8 us
    ppermute x3, waiting for transfers between devices, halving_scatter(): x = keep + lax.ppermute(send, axis, [(i, i ^ bit) for i in range(size)])  18.8 us
    gather x1, local copies, waits for them, and re-layouts, per_device(): source_rows = gathered[source_index]  15.1 us
    pallas_call x1, Pallas kernels, chol_basis(): pl.pallas_call(chol_kernel, out_shape=jax.ShapeDtypeStruct((count, R, K),...  11.5 us
    ppermute x3, starting transfers between devices, halving_scatter(): x = keep + lax.ppermute(send, axis, [(i, i ^ bit) for i in range(size)])  4.77 us
    pallas_call x1, Pallas kernels, local_gram(): pl.pallas_call(gram_kernel, grid=(count // tile,), in_specs=[pl.BlockSpec...  4.61 us
  transfers between devices with their start and end apart: 4, of which 4 were waited for; matrix products, arithmetic and copies ran while one was open for 4% of the time, Pallas kernels for 5%

profile of v7, /device:TPU:1, one launch (start us, length us, event | category | flops | bytes accessed | tf_op | source)
XLA Modules:
  0.0 220.3 jit_solution(8318950697746114339)
XLA Ops:
  6.5 0.0 copy-start
  6.5 0.0 all-gather.3.cloned.1.call-start
  6.5 4.6 %shard_map.73 = f32[64,64,64]{2,1,0:T(8,128)} custom-call(bf16[64,16384]{1,0:T(8,128)(2,1)} %x_ref.1), custom_call_target="tpu_custom_call" | custom-call | tf_op jit(solution)/shard_map/pallas_call | solution.py:111
  11.2 0.0 copy-start.1
  11.2 2.5 %constant_dynamic-slice_fusion.7 = f32[32,64,64]{2,1,0:T(8,128)} fusion(f32[64,64,64]{2,1,0:T(8,128)} %shard_map.73, s32[]{:T(128)S(6)} %select_n.103), kind=kLoop, calls=%fused_computation.49 | loop fusion | bytes 1048580 | tf_op jit(solution)/shard_map/dynamic_slice | solution.py:128
  13.6 3.2 %collective-permute-start = (f32[32,64,64]{2,1,0:T(8,128)}, f32[32,64,64]{2,1,0:T(8,128)}, u32[]{:S(2)}, u32[]{:S(2)}) collective-permute-start(f32[32,64,64]{2,1,0:T(8,128)} %constant_dynamic-slice_fusion.7), channel_id=1, source_target_pairs={{0,4},{4,0},{1,5},{5,1},{2,6},{6,2},{3,7},{7,3},{8,12},{12,8},{9,1... | collective-permute-start | bytes 1572872 | tf_op jit(solution)/shard_map/ppermute | solution.py:129
  16.8 0.0 copy-done
  16.8 0.8 constant_dynamic-slice_fusion.1
  17.7 1.8 collective-permute-done
  19.4 0.0 copy-done.1
  19.4 1.4 dynamic-slice_add_fusion
  20.8 0.0 copy-start.2
  20.8 1.0 copy-done.2
  21.8 1.3 collective-permute-start.1
  23.1 0.8 constant_dynamic-slice_fusion
  23.9 0.1 slice.18
  24.0 0.2 slice.17
  24.2 0.8 constant_dynamic-slice_fusion.2
  25.0 11.5 %collective-permute-done.1 = f32[16,64,64]{2,1,0:T(8,128)S(1)} collective-permute-done((f32[16,64,64]{2,1,0:T(8,128)S(1)}, f32[16,64,64]{2,1,0:T(8,128)S(1)}, u32[]{:S(2)}, u32[]{:S(2)}) %collective-permute-start.1) | collective-permute-done | bytes 262176 | tf_op jit(solution)/shard_map/ppermute | solution.py:129
  36.5 1.1 dynamic-slice_add_fusion.1
  37.7 0.3 collective-permute-start.2
  38.0 0.0 copy-start.5
  38.0 0.0 copy-start.3
  38.0 0.0 copy-start.4
  38.0 0.2 reshape.36
  38.2 0.9 copy.13
  39.0 5.5 %collective-permute-done.2 = f32[8,64,64]{2,1,0:T(8,128)S(1)} collective-permute-done((f32[8,64,64]{2,1,0:T(8,128)S(1)}, f32[8,64,64]{2,1,0:T(8,128)S(1)}, u32[]{:S(2)}, u32[]{:S(2)}) %collective-permute-start.2) | collective-permute-done | bytes 131104 | tf_op jit(solution)/shard_map/ppermute | solution.py:129
  44.6 0.3 fusion.10
  44.9 0.3 bitcast_reduce_fusion
  45.2 0.3 fusion.11
  45.4 0.2 bitcast_reduce_fusion.1
  45.6 0.8 pad_maximum_fusion.g_ref
  46.5 11.5 %shard_map.74 = f32[14,32,64]{2,1,0:T(8,128)} custom-call(f32[14,64,64]{2,1,0:T(8,128)} %pad_maximum_fusion.g_ref, f32[14,32,64]{2,1,0:T(8,128)} %bitcast.15), custom_call_target="tpu_custom_call" | custom-call | tf_op jit(solution)/shard_map/pallas_call | solution.py:57
  58.0 1.0 convert_element_type.11
  58.9 0.1 reshape.31
  59.1 0.6 pad.4
  59.7 0.0 all-gather.3.cloned.1.call-update
  59.8 0.0 copy-done.5
  59.8 0.0 copy-done.3
  59.8 0.0 copy-done.4
  59.8 0.3 compare_select_fusion
  60.1 0.1 reshape.55
  60.2 24.6 %all-gather = bf16[8,14,2048]{2,1,0:T(8,128)(2,1)S(1)} all-gather(bf16[1,14,2048]{2,1,0:T(8,128)(2,1)S(1)} %reshape.55), channel_id=1, replica_groups=mesh['leaf'=32,'basis'=2,'coup'=4] {'basis','coup'}, dimensions={0}, use_global_device_ids=true | all-gather | bytes 516096 | tf_op jit(solution)/shard_map/all_gather | solution.py:159
  84.8 0.1 slice.28
  85.1 4.2 %gather_fusion = bf16[768,2048]{1,0:T(8,128)(2,1)} fusion(bf16[112,2048]{1,0:T(8,128)(2,1)S(1)} %pad_maximum_fusion.1, s32[1024]{0:T(1024)S(1)} %pad_clamp_fusion.1), kind=kCustom, calls=%fused_computation | custom fusion | bytes 6294528 | tf_op jit(solution)/shard_map/gather | solution.py:170
  89.3 11.7 %shard_map.75.l_ref = bf16[768,2048]{1,0:T(8,128)(2,1)} custom-call(bf16[768,2048]{1,0:T(8,128)(2,1)} %gather_fusion, bf16[768,4096]{1,0:T(8,128)(2,1)} %s_ref.1), custom_call_target="tpu_custom_call" | custom-call | tf_op jit(solution)/shard_map/pallas_call | solution.py:85
  101.0 87.2 %all-gather.3.cloned.1.call-done = bf16[4096,2048]{1,0:T(8,128)(2,1)} async-done(((bf16[16,2048]{1,0:T(8,128)(2,1)}), bf16[4096,2048]{1,0:T(8,128)(2,1)}) %all-gather.3.cloned.1.call-update) | async-done | bytes 16777232 | tf_op jit(solution)/shard_map/all_gather | solution.py:178
  188.2 15.1 %gather_fusion.1 = bf16[768,2048]{1,0:T(8,128)(2,1)} fusion(bf16[4096,2048]{1,0:T(8,128)(2,1)} %all-gather.3.cloned.1.call-done, s32[1024]{0:T(1024)S(1)} %pad_clamp_fusion), kind=kCustom, calls=%fused_computation.1 | custom fusion | bytes 6294528 | tf_op jit(solution)/shard_map/gather | solution.py:179
  203.2 10.2 %shard_map.76 = f32[768,1024]{1,0:T(8,128)} custom-call(bf16[768,2048]{1,0:T(8,128)(2,1)} %shard_map.75.l_ref, bf16[768,2048]{1,0:T(8,128)(2,1)} %gather_fusion.1), custom_call_target="tpu_custom_call" | custom-call | tf_op jit(solution)/shard_map/pallas_call | solution.py:85
  (14 shorter events, 0.3 us)
Async XLA Ops:
  6.5 10.3 %copy-start = (bf16[96,4096]{1,0:T(8,128)(2,1)S(1)}, bf16[96,4096]{1,0:T(8,128)(2,1)}, u32[]{:S(2)}) copy-start(bf16[96,4096]{1,0:T(8,128)(2,1)} %param.8) | copy-start | bytes 2359300
  6.5 181.7 %all-gather.3.cloned.1.call-start = ((), (), s32[]{:S(2)}) async-start(), calls=%async_computation | async-start | bytes 16842752 | tf_op jit(solution)/shard_map/all_gather | solution.py:178
  11.2 8.3 %copy-start.1 = (f32[64,64,64]{2,1,0:T(8,128)S(1)}, f32[64,64,64]{2,1,0:T(8,128)}, u32[]{:S(2)}) copy-start(f32[64,64,64]{2,1,0:T(8,128)} %shard_map.73) | copy-start | bytes 3145732
  13.6 5.8 %collective-permute-start = (f32[32,64,64]{2,1,0:T(8,128)}, f32[32,64,64]{2,1,0:T(8,128)}, u32[]{:S(2)}, u32[]{:S(2)}) collective-permute-start(f32[32,64,64]{2,1,0:T(8,128)} %constant_dynamic-slice_fusion.7), channel_id=1, source_target_pairs={{0,4},{4,0},{1,5},{5,1},{2,6},{6,2},{3,7},{7,3},{8,12},{12,8},{9,1... | collective-permute-start | bytes 1572872 | tf_op jit(solution)/shard_map/ppermute | solution.py:129
  20.8 1.0 copy-start.2
  21.8 14.7 %collective-permute-start.1 = (f32[16,64,64]{2,1,0:T(8,128)S(1)}, f32[16,64,64]{2,1,0:T(8,128)S(1)}, u32[]{:S(2)}, u32[]{:S(2)}) collective-permute-start(f32[16,64,64]{2,1,0:T(8,128)S(1)} %constant_dynamic-slice_fusion.6), channel_id=1, source_target_pairs={{0,2},{1,3},{2,0},{3,1},{4,6},{5,7},{6,4},{7,5},{8,10},{9,11},{10,... | collective-permute-start | bytes 786440 | tf_op jit(solution)/shard_map/ppermute | solution.py:129
  37.7 6.9 %collective-permute-start.2 = (f32[8,64,64]{2,1,0:T(8,128)S(1)}, f32[8,64,64]{2,1,0:T(8,128)S(1)}, u32[]{:S(2)}, u32[]{:S(2)}) collective-permute-start(f32[8,64,64]{2,1,0:T(8,128)S(1)} %constant_dynamic-slice_fusion.5), channel_id=1, source_target_pairs={{0,1},{1,0},{2,3},{3,2},{4,5},{5,4},{6,7},{7,6},{8,9},{9,8},{10,11... | collective-permute-start | bytes 393224 | tf_op jit(solution)/shard_map/ppermute | solution.py:129
  38.0 21.8 %copy-start.5 = (s32[768,1]{0,1:T(1,128)S(1)}, s32[768,1]{0,1:T(1,128)}, u32[]{:S(2)}) copy-start(s32[768,1]{0,1:T(1,128)} %param.12) | copy-start | bytes 9220
  38.0 21.8 %copy-start.3 = (s32[768]{0:T(1024)S(1)}, s32[768]{0:T(1024)}, u32[]{:S(2)}) copy-start(s32[768]{0:T(1024)} %param.13) | copy-start | bytes 9220
  38.0 21.8 %copy-start.4 = (s32[768]{0:T(1024)S(1)}, s32[768]{0:T(1024)}, u32[]{:S(2)}) copy-start(s32[768]{0:T(1024)} %param.11) | copy-start | bytes 9220
Sparse Core Ops, SparseCore 0:
  59.9 128.2 all-gather.2

commit v8 on v7

--- a/solution.py
+++ b/solution.py
@@ -102,7 +102,10 @@
 def gram_kernel(x_ref, o_ref):
     tile = x_ref.shape[0]
     rows = x_ref[...].reshape(tile, -1, K)
-    o_ref[...] = jnp.einsum("nik,nil->nkl", rows, rows, preferred_element_type=jnp.float32)
+    gram = jnp.einsum("nik,nil->nkl", rows, rows, preferred_element_type=jnp.float32)
+    part = tile // 4
+    for c, dst in enumerate((0, 2, 1, 3)):
+        o_ref[dst * part : (dst + 1) * part] = gram[c * part : (c + 1) * part]
 
 
 def local_gram(basis_rows):
@@ -119,7 +122,7 @@
 
 def halving_scatter(x):
     coup_size = lax.axis_size("coup")
-    steps = [("basis", 1)] + [("coup", bit) for bit in (2, 1) if bit < coup_size]
+    steps = [("basis", 1)] + [("coup", bit) for bit in (1, 2) if bit < coup_size]
     for axis, bit in steps:
         size = lax.axis_size(axis)
         mine = (lax.axis_index(axis) // bit) % 2

time: 221 us -> 218 us (0.986)
  no operation moved by 1% of the time
where the time goes in v8:
time: 218 us; the launch traced here: 217 us
  waiting for transfers between devices  106 us (49%)
  Pallas kernels  38 us (17%)
  local copies, waits for them, and re-layouts  25.5 us (12%)
  blocking collectives  24.6 us (11%)
  between operations  13.7 us (6%)
  starting transfers between devices  4.86 us (2%)
  other arithmetic  3.61 us (2%)
    all_gather x1, waiting for transfers between devices, per_device(): lax.all_gather(padded_table, ('leaf', 'basis', 'coup'), axis=0, tiled=True)  87.2 us
    all_gather x1, blocking collectives, per_device(): lax.all_gather(local_table, ('basis', 'coup'), axis=0, tiled=True)  24.6 us
    pallas_call x2, Pallas kernels, row_tiled(): pl.pallas_call(kernel, grid=(count // tile,), in_specs=[pl.BlockSpec((til...  21.8 us
    ppermute x3, waiting for transfers between devices, halving_scatter(): x = keep + lax.ppermute(send, axis, [(i, i ^ bit) for i in range(size)])  18.5 us
    gather x1, local copies, waits for them, and re-layouts, per_device(): source_rows = gathered[source_index]  15 us
    pallas_call x1, Pallas kernels, chol_basis(): pl.pallas_call(chol_kernel, out_shape=jax.ShapeDtypeStruct((count, R, K),...  11.5 us
    ppermute x3, starting transfers between devices, halving_scatter(): x = keep + lax.ppermute(send, axis, [(i, i ^ bit) for i in range(size)])  4.85 us
    pallas_call x1, Pallas kernels, local_gram(): pl.pallas_call(gram_kernel, grid=(count // tile,), in_specs=[pl.BlockSpec...  4.61 us
  transfers between devices with their start and end apart: 4, of which 4 were waited for; matrix products, arithmetic and copies ran while one was open for 4% of the time, Pallas kernels for 5%

profile of v8, /device:TPU:1, one launch (start us, length us, event | category | flops | bytes accessed | tf_op | source)
XLA Modules:
  0.0 216.9 jit_solution(2810363386901460935)
XLA Ops:
  6.5 0.0 copy-start
  6.5 0.0 all-gather.3.cloned.1.call-start
  6.5 4.6 %shard_map.73 = f32[64,64,64]{2,1,0:T(8,128)} custom-call(bf16[64,16384]{1,0:T(8,128)(2,1)} %x_ref.1), custom_call_target="tpu_custom_call" | custom-call | tf_op jit(solution)/shard_map/pallas_call | solution.py:114
  11.2 1.3 constant_dynamic-slice_fusion.7
  12.5 3.3 %collective-permute-start = (f32[32,64,64]{2,1,0:T(8,128)S(1)}, f32[32,64,64]{2,1,0:T(8,128)S(1)}, u32[]{:S(2)}, u32[]{:S(2)}) collective-permute-start(f32[32,64,64]{2,1,0:T(8,128)S(1)} %constant_dynamic-slice_fusion.7), channel_id=1, source_target_pairs={{0,4},{4,0},{1,5},{5,1},{2,6},{6,2},{3,7},{7,3},{8,12},{12,8},{9,1... | collective-permute-start | bytes 1572872 | tf_op jit(solution)/shard_map/ppermute | solution.py:132
  15.8 0.0 copy-done
  15.8 0.8 constant_dynamic-slice_fusion.1
  16.6 1.4 collective-permute-done
  18.1 1.4 dynamic-slice_add_fusion
  19.5 0.1 collective-permute-start.1
  19.6 0.8 constant_dynamic-slice_fusion
  20.4 0.1 slice.18
  20.6 0.2 slice.17
  20.8 0.8 constant_dynamic-slice_fusion.2
  21.5 11.2 %collective-permute-done.1 = f32[16,64,64]{2,1,0:T(8,128)S(1)} collective-permute-done((f32[16,64,64]{2,1,0:T(8,128)S(1)}, f32[16,64,64]{2,1,0:T(8,128)S(1)}, u32[]{:S(2)}, u32[]{:S(2)}) %collective-permute-start.1) | collective-permute-done | bytes 262176 | tf_op jit(solution)/shard_map/ppermute | solution.py:132
  32.7 0.1 dynamic-slice_add_fusion.1
  32.8 1.5 collective-permute-start.2
  34.3 0.0 copy-start.3
  34.3 0.0 copy-start.1
  34.4 0.0 copy-start.2
  34.4 0.2 reshape.36
  34.5 0.9 copy.13
  35.4 5.9 %collective-permute-done.2 = f32[8,64,64]{2,1,0:T(8,128)S(1)} collective-permute-done((f32[8,64,64]{2,1,0:T(8,128)S(1)}, f32[8,64,64]{2,1,0:T(8,128)S(1)}, u32[]{:S(2)}, u32[]{:S(2)}) %collective-permute-start.2) | collective-permute-done | bytes 131104 | tf_op jit(solution)/shard_map/ppermute | solution.py:132
  41.3 0.3 fusion.10
  41.6 0.3 bitcast_reduce_fusion
  41.8 0.3 fusion.11
  42.1 0.2 bitcast_reduce_fusion.1
  42.3 0.8 pad_maximum_fusion.g_ref
  43.1 11.5 %shard_map.74 = f32[14,32,64]{2,1,0:T(8,128)} custom-call(f32[14,64,64]{2,1,0:T(8,128)} %pad_maximum_fusion.g_ref, f32[14,32,64]{2,1,0:T(8,128)} %bitcast.15), custom_call_target="tpu_custom_call" | custom-call | tf_op jit(solution)/shard_map/pallas_call | solution.py:57
  54.7 1.0 convert_element_type.11
  55.6 0.1 reshape.31
  55.8 0.6 pad.4
  56.4 0.0 all-gather.3.cloned.1.call-update
  56.4 0.0 copy-done.3
  56.5 0.0 copy-done.1
  56.5 0.0 copy-done.2
  56.5 0.3 compare_select_fusion
  56.8 0.1 reshape.55
  56.9 24.6 %all-gather = bf16[8,14,2048]{2,1,0:T(8,128)(2,1)S(1)} all-gather(bf16[1,14,2048]{2,1,0:T(8,128)(2,1)S(1)} %reshape.55), channel_id=1, replica_groups=mesh['leaf'=32,'basis'=2,'coup'=4] {'basis','coup'}, dimensions={0}, use_global_device_ids=true | all-gather | bytes 516096 | tf_op jit(solution)/shard_map/all_gather | solution.py:162
  81.5 0.1 slice.28
  81.8 4.2 %gather_fusion = bf16[768,2048]{1,0:T(8,128)(2,1)} fusion(bf16[112,2048]{1,0:T(8,128)(2,1)S(1)} %pad_maximum_fusion.1, s32[1024]{0:T(1024)S(1)} %pad_clamp_fusion.1), kind=kCustom, calls=%fused_computation | custom fusion | bytes 6294528 | tf_op jit(solution)/shard_map/gather | solution.py:173
  86.0 11.6 %shard_map.75.l_ref = bf16[768,2048]{1,0:T(8,128)(2,1)} custom-call(bf16[768,2048]{1,0:T(8,128)(2,1)} %gather_fusion, bf16[768,4096]{1,0:T(8,128)(2,1)} %s_ref.1), custom_call_target="tpu_custom_call" | custom-call | tf_op jit(solution)/shard_map/pallas_call | solution.py:85
  97.6 87.2 %all-gather.3.cloned.1.call-done = bf16[4096,2048]{1,0:T(8,128)(2,1)} async-done(((bf16[16,2048]{1,0:T(8,128)(2,1)}), bf16[4096,2048]{1,0:T(8,128)(2,1)}) %all-gather.3.cloned.1.call-update) | async-done | bytes 16777232 | tf_op jit(solution)/shard_map/all_gather | solution.py:181
  184.9 15.0 %gather_fusion.1 = bf16[768,2048]{1,0:T(8,128)(2,1)} fusion(bf16[4096,2048]{1,0:T(8,128)(2,1)} %all-gather.3.cloned.1.call-done, s32[1024]{0:T(1024)S(1)} %pad_clamp_fusion), kind=kCustom, calls=%fused_computation.1 | custom fusion | bytes 6294528 | tf_op jit(solution)/shard_map/gather | solution.py:182
  199.9 10.2 %shard_map.76 = f32[768,1024]{1,0:T(8,128)} custom-call(bf16[768,2048]{1,0:T(8,128)(2,1)} %shard_map.75.l_ref, bf16[768,2048]{1,0:T(8,128)(2,1)} %gather_fusion.1), custom_call_target="tpu_custom_call" | custom-call | tf_op jit(solution)/shard_map/pallas_call | solution.py:85
  (14 shorter events, 0.3 us)
Async XLA Ops:
  6.5 9.2 %copy-start = (bf16[96,4096]{1,0:T(8,128)(2,1)S(1)}, bf16[96,4096]{1,0:T(8,128)(2,1)}, u32[]{:S(2)}) copy-start(bf16[96,4096]{1,0:T(8,128)(2,1)} %param.8) | copy-start | bytes 2359300
  6.5 178.3 %all-gather.3.cloned.1.call-start = ((), (), s32[]{:S(2)}) async-start(), calls=%async_computation | async-start | bytes 16842752 | tf_op jit(solution)/shard_map/all_gather | solution.py:181
  12.5 5.6 %collective-permute-start = (f32[32,64,64]{2,1,0:T(8,128)S(1)}, f32[32,64,64]{2,1,0:T(8,128)S(1)}, u32[]{:S(2)}, u32[]{:S(2)}) collective-permute-start(f32[32,64,64]{2,1,0:T(8,128)S(1)} %constant_dynamic-slice_fusion.7), channel_id=1, source_target_pairs={{0,4},{4,0},{1,5},{5,1},{2,6},{6,2},{3,7},{7,3},{8,12},{12,8},{9,1... | collective-permute-start | bytes 1572872 | tf_op jit(solution)/shard_map/ppermute | solution.py:132
  19.5 13.2 %collective-permute-start.1 = (f32[16,64,64]{2,1,0:T(8,128)S(1)}, f32[16,64,64]{2,1,0:T(8,128)S(1)}, u32[]{:S(2)}, u32[]{:S(2)}) collective-permute-start(f32[16,64,64]{2,1,0:T(8,128)S(1)} %constant_dynamic-slice_fusion.6), channel_id=1, source_target_pairs={{0,1},{1,0},{2,3},{3,2},{4,5},{5,4},{6,7},{7,6},{8,9},{9,8},{10,11... | collective-permute-start | bytes 786440 | tf_op jit(solution)/shard_map/ppermute | solution.py:132
  32.8 8.4 %collective-permute-start.2 = (f32[8,64,64]{2,1,0:T(8,128)S(1)}, f32[8,64,64]{2,1,0:T(8,128)S(1)}, u32[]{:S(2)}, u32[]{:S(2)}) collective-permute-start(f32[8,64,64]{2,1,0:T(8,128)S(1)} %constant_dynamic-slice_fusion.5), channel_id=1, source_target_pairs={{0,2},{1,3},{2,0},{3,1},{4,6},{5,7},{6,4},{7,5},{8,10},{9,11},{10,... | collective-permute-start | bytes 393224 | tf_op jit(solution)/shard_map/ppermute | solution.py:132
  34.3 22.1 %copy-start.3 = (s32[768,1]{0,1:T(1,128)S(1)}, s32[768,1]{0,1:T(1,128)}, u32[]{:S(2)}) copy-start(s32[768,1]{0,1:T(1,128)} %param.12) | copy-start | bytes 9220
  34.3 22.1 %copy-start.1 = (s32[768]{0:T(1024)S(1)}, s32[768]{0:T(1024)}, u32[]{:S(2)}) copy-start(s32[768]{0:T(1024)} %param.13) | copy-start | bytes 9220
  34.4 22.1 %copy-start.2 = (s32[768]{0:T(1024)S(1)}, s32[768]{0:T(1024)}, u32[]{:S(2)}) copy-start(s32[768]{0:T(1024)} %param.11) | copy-start | bytes 9220
Sparse Core Ops, SparseCore 0:
  56.5 128.2 all-gather.2

commit v9 on v8

--- a/solution.py
+++ b/solution.py
@@ -31,8 +31,7 @@
         levels.append(gram_now)
     gram_all = jnp.concatenate(levels, axis=0)
     sketch_t = omega.reshape(-1, K, R).astype(jnp.float32).transpose(0, 2, 1)
-    basis_table = chol_basis(gram_all, sketch_t)
-    return basis_table.astype(jnp.bfloat16).reshape(-1, R * K)
+    return chol_basis(gram_all, sketch_t)
 
 
 def chol_kernel(g_ref, om_ref, out_ref, lt_ref):
@@ -46,17 +45,20 @@
         lt_ref[:, j : j + 1, :] = scaled
         col = a[:, :, j : j + 1] * inv
         a = a - col * scaled
-    out_ref[...] = jnp.einsum(
+    basis = jnp.einsum(
         "nrk,nkj->nrj", om_ref[...], lt_ref[...], precision=lax.Precision.HIGHEST,
         preferred_element_type=jnp.float32,
     )
+    out_ref[:count] = basis.astype(jnp.bfloat16).reshape(count, R * K)
+    out_ref[count:] = jnp.zeros((out_ref.shape[0] - count, R * K), jnp.bfloat16)
 
 
 def chol_basis(gram_all, sketch_t):
     count = gram_all.shape[0]
+    padded = -(-count // 8) * 8 + (8 if count % 8 == 0 else 0)
     return pl.pallas_call(
         chol_kernel,
-        out_shape=jax.ShapeDtypeStruct((count, R, K), jnp.float32),
+        out_shape=jax.ShapeDtypeStruct((padded, R * K), jnp.bfloat16),
         scratch_shapes=[pltpu.VMEM((count, K, K), jnp.float32)],
     )(gram_all, sketch_t)
 
@@ -158,7 +160,8 @@
         ],
         axis=0,
     )
-    local_table = upsweep(gram_share, links_local, sketch_local, local_count)
+    padded_table = upsweep(gram_share, links_local, sketch_local, local_count)
+    local_table = padded_table[: local_count + half_count + quarter_count]
     collected = lax.all_gather(local_table, ("basis", "coup"), axis=0, tiled=True)
     collected = collected.reshape(group, local_count + half_count + quarter_count, R * K)
     basis_table = jnp.concatenate(
@@ -171,8 +174,7 @@
     )
     slots_per_leaf = basis_table.shape[0]
     left_rows = left_product(basis_table[block_target], blocks)
-    local_rows = -(-local_table.shape[0] // 8) * 8
-    padded_table = jnp.pad(local_table, ((0, local_rows - local_table.shape[0]), (0, 0)))
+    local_rows = padded_table.shape[0]
     base, node_count = level_slots(block_target)
     within = source_offset % node_count
     per_member = node_count // group

time: 218 us -> 216 us (level)
  no operation moved by 1% of the time
where the time goes in v9:
time: 216 us; the launch traced here: 215 us
  waiting for transfers between devices  105 us (49%)
  Pallas kernels  37.9 us (18%)
  local copies, waits for them, and re-layouts  25.4 us (12%)
  blocking collectives  24.5 us (11%)
  between operations  13.7 us (6%)
  starting transfers between devices  4.86 us (2%)
  other arithmetic  2.65 us (1%)
    all_gather x1, waiting for transfers between devices, per_device(): lax.all_gather(padded_table, ('leaf', 'basis', 'coup'), axis=0, tiled=True)  86.7 us
    all_gather x1, blocking collectives, per_device(): lax.all_gather(local_table, ('basis', 'coup'), axis=0, tiled=True)  24.5 us
    pallas_call x2, Pallas kernels, row_tiled(): pl.pallas_call(kernel, grid=(count // tile,), in_specs=[pl.BlockSpec((til...  21.8 us
    ppermute x3, waiting for transfers between devices, halving_scatter(): x = keep + lax.ppermute(send, axis, [(i, i ^ bit) for i in range(size)])  18.5 us
    gather x1, local copies, waits for them, and re-layouts, per_device(): source_rows = gathered[source_index]  15 us
    pallas_call x1, Pallas kernels, chol_basis(): pl.pallas_call(chol_kernel, out_shape=jax.ShapeDtypeStruct((padded, R * K...  11.5 us
    ppermute x3, starting transfers between devices, halving_scatter(): x = keep + lax.ppermute(send, axis, [(i, i ^ bit) for i in range(size)])  4.85 us
    pallas_call x1, Pallas kernels, local_gram(): pl.pallas_call(gram_kernel, grid=(count // tile,), in_specs=[pl.BlockSpec...  4.61 us
  transfers between devices with their start and end apart: 4, of which 4 were waited for; matrix products, arithmetic and copies ran while one was open for 4% of the time, Pallas kernels for 5%

profile of v9, /device:TPU:1, one launch (start us, length us, event | category | flops | bytes accessed | tf_op | source)
XLA Modules:
  0.0 215.3 jit_solution(8241796661032907053)
XLA Ops:
  6.5 0.0 copy-start
  6.5 0.0 all-gather.3.cloned.1.call-start
  6.5 4.6 %shard_map.73 = f32[64,64,64]{2,1,0:T(8,128)} custom-call(bf16[64,16384]{1,0:T(8,128)(2,1)} %x_ref.1), custom_call_target="tpu_custom_call" | custom-call | tf_op jit(solution)/shard_map/pallas_call | solution.py:116
  11.2 1.3 constant_dynamic-slice_fusion.7
  12.5 3.3 %collective-permute-start = (f32[32,64,64]{2,1,0:T(8,128)S(1)}, f32[32,64,64]{2,1,0:T(8,128)S(1)}, u32[]{:S(2)}, u32[]{:S(2)}) collective-permute-start(f32[32,64,64]{2,1,0:T(8,128)S(1)} %constant_dynamic-slice_fusion.7), channel_id=1, source_target_pairs={{0,4},{4,0},{1,5},{5,1},{2,6},{6,2},{3,7},{7,3},{8,12},{12,8},{9,1... | collective-permute-start | bytes 1572872 | tf_op jit(solution)/shard_map/ppermute | solution.py:134
  15.8 0.0 copy-done
  15.8 0.8 constant_dynamic-slice_fusion.1
  16.6 1.4 collective-permute-done
  18.1 1.4 dynamic-slice_add_fusion
  19.5 0.1 collective-permute-start.1
  19.6 0.8 constant_dynamic-slice_fusion
  20.4 0.1 slice.21
  20.6 0.2 slice.20
  20.8 0.8 constant_dynamic-slice_fusion.2
  21.5 11.2 %collective-permute-done.1 = f32[16,64,64]{2,1,0:T(8,128)S(1)} collective-permute-done((f32[16,64,64]{2,1,0:T(8,128)S(1)}, f32[16,64,64]{2,1,0:T(8,128)S(1)}, u32[]{:S(2)}, u32[]{:S(2)}) %collective-permute-start.1) | collective-permute-done | bytes 262176 | tf_op jit(solution)/shard_map/ppermute | solution.py:134
  32.7 0.1 dynamic-slice_add_fusion.1
  32.8 0.0 copy-start.3
  32.8 0.0 copy-start.1
  32.8 0.0 copy-start.2
  32.9 1.5 collective-permute-start.2
  34.4 0.2 reshape.32
  34.5 0.9 copy.13
  35.4 5.9 %collective-permute-done.2 = f32[8,64,64]{2,1,0:T(8,128)S(1)} collective-permute-done((f32[8,64,64]{2,1,0:T(8,128)S(1)}, f32[8,64,64]{2,1,0:T(8,128)S(1)}, u32[]{:S(2)}, u32[]{:S(2)}) %collective-permute-start.2) | collective-permute-done | bytes 131104 | tf_op jit(solution)/shard_map/ppermute | solution.py:134
  41.3 0.3 fusion.10
  41.6 0.3 bitcast_reduce_fusion
  41.9 0.3 fusion.11
  42.1 0.2 bitcast_reduce_fusion.1
  42.4 0.8 pad_maximum_fusion.g_ref
  43.2 11.5 %shard_map.74 = bf16[16,2048]{1,0:T(8,128)(2,1)} custom-call(f32[14,64,64]{2,1,0:T(8,128)} %pad_maximum_fusion.g_ref, f32[14,32,64]{2,1,0:T(8,128)} %bitcast.17), custom_call_target="tpu_custom_call" | custom-call | tf_op jit(solution)/shard_map/pallas_call | solution.py:59
  54.7 0.0 all-gather.3.cloned.1.call-update
  54.7 0.0 copy-done.3
  54.7 0.0 copy-done.1
  54.7 0.0 copy-done.2
  54.7 0.3 compare_select_fusion
  55.0 0.8 slice_bitcast_fusion.1
  55.9 24.5 %all-gather = bf16[8,14,2048]{2,1,0:T(8,128)(2,1)S(1)} all-gather(bf16[1,14,2048]{2,1,0:T(8,128)(2,1)S(1)} %slice_bitcast_fusion.1), channel_id=1, replica_groups=mesh['leaf'=32,'basis'=2,'coup'=4] {'basis','coup'}, dimensions={0}, use_global_device_ids=true | all-gather | bytes 516096 | tf_op jit(solution)/shard_map/all_gather | solution.py:165
  80.4 0.1 slice.33
  80.6 4.2 %gather_fusion = bf16[768,2048]{1,0:T(8,128)(2,1)} fusion(bf16[112,2048]{1,0:T(8,128)(2,1)S(1)} %pad_maximum_fusion.1, s32[1024]{0:T(1024)S(1)} %pad_clamp_fusion.1), kind=kCustom, calls=%fused_computation | custom fusion | bytes 6294528 | tf_op jit(solution)/shard_map/gather | solution.py:176
  84.9 11.6 %shard_map.75.l_ref = bf16[768,2048]{1,0:T(8,128)(2,1)} custom-call(bf16[768,2048]{1,0:T(8,128)(2,1)} %gather_fusion, bf16[768,4096]{1,0:T(8,128)(2,1)} %s_ref.1), custom_call_target="tpu_custom_call" | custom-call | tf_op jit(solution)/shard_map/pallas_call | solution.py:87
  96.5 86.7 %all-gather.3.cloned.1.call-done = bf16[4096,2048]{1,0:T(8,128)(2,1)} async-done(((bf16[16,2048]{1,0:T(8,128)(2,1)}), bf16[4096,2048]{1,0:T(8,128)(2,1)}) %all-gather.3.cloned.1.call-update) | async-done | bytes 16777232 | tf_op jit(solution)/shard_map/all_gather | solution.py:183
  183.2 15.0 %gather_fusion.1 = bf16[768,2048]{1,0:T(8,128)(2,1)} fusion(bf16[4096,2048]{1,0:T(8,128)(2,1)} %all-gather.3.cloned.1.call-done, s32[1024]{0:T(1024)S(1)} %pad_clamp_fusion), kind=kCustom, calls=%fused_computation.1 | custom fusion | bytes 6294528 | tf_op jit(solution)/shard_map/gather | solution.py:184
  198.2 10.2 %shard_map.76 = f32[768,1024]{1,0:T(8,128)} custom-call(bf16[768,2048]{1,0:T(8,128)(2,1)} %shard_map.75.l_ref, bf16[768,2048]{1,0:T(8,128)(2,1)} %gather_fusion.1), custom_call_target="tpu_custom_call" | custom-call | tf_op jit(solution)/shard_map/pallas_call | solution.py:87
  (14 shorter events, 0.3 us)
Async XLA Ops:
  6.5 9.2 %copy-start = (bf16[96,4096]{1,0:T(8,128)(2,1)S(1)}, bf16[96,4096]{1,0:T(8,128)(2,1)}, u32[]{:S(2)}) copy-start(bf16[96,4096]{1,0:T(8,128)(2,1)} %param.8) | copy-start | bytes 2359300
  6.5 176.7 %all-gather.3.cloned.1.call-start = ((), (), s32[]{:S(2)}) async-start(), calls=%async_computation | async-start | bytes 16842752 | tf_op jit(solution)/shard_map/all_gather | solution.py:183
  12.5 5.6 %collective-permute-start = (f32[32,64,64]{2,1,0:T(8,128)S(1)}, f32[32,64,64]{2,1,0:T(8,128)S(1)}, u32[]{:S(2)}, u32[]{:S(2)}) collective-permute-start(f32[32,64,64]{2,1,0:T(8,128)S(1)} %constant_dynamic-slice_fusion.7), channel_id=1, source_target_pairs={{0,4},{4,0},{1,5},{5,1},{2,6},{6,2},{3,7},{7,3},{8,12},{12,8},{9,1... | collective-permute-start | bytes 1572872 | tf_op jit(solution)/shard_map/ppermute | solution.py:134
  19.5 13.2 %collective-permute-start.1 = (f32[16,64,64]{2,1,0:T(8,128)S(1)}, f32[16,64,64]{2,1,0:T(8,128)S(1)}, u32[]{:S(2)}, u32[]{:S(2)}) collective-permute-start(f32[16,64,64]{2,1,0:T(8,128)S(1)} %constant_dynamic-slice_fusion.6), channel_id=1, source_target_pairs={{0,1},{1,0},{2,3},{3,2},{4,5},{5,4},{6,7},{7,6},{8,9},{9,8},{10,11... | collective-permute-start | bytes 786440 | tf_op jit(solution)/shard_map/ppermute | solution.py:134
  32.8 21.9 %copy-start.3 = (s32[768,1]{0,1:T(1,128)S(1)}, s32[768,1]{0,1:T(1,128)}, u32[]{:S(2)}) copy-start(s32[768,1]{0,1:T(1,128)} %param.12) | copy-start | bytes 9220
  32.8 21.9 %copy-start.1 = (s32[768]{0:T(1024)S(1)}, s32[768]{0:T(1024)}, u32[]{:S(2)}) copy-start(s32[768]{0:T(1024)} %param.13) | copy-start | bytes 9220
  32.8 21.9 %copy-start.2 = (s32[768]{0:T(1024)S(1)}, s32[768]{0:T(1024)}, u32[]{:S(2)}) copy-start(s32[768]{0:T(1024)} %param.11) | copy-start | bytes 9220
  32.9 8.4 %collective-permute-start.2 = (f32[8,64,64]{2,1,0:T(8,128)S(1)}, f32[8,64,64]{2,1,0:T(8,128)S(1)}, u32[]{:S(2)}, u32[]{:S(2)}) collective-permute-start(f32[8,64,64]{2,1,0:T(8,128)S(1)} %constant_dynamic-slice_fusion.5), channel_id=1, source_target_pairs={{0,2},{1,3},{2,0},{3,1},{4,6},{5,7},{6,4},{7,5},{8,10},{9,11},{10,... | collective-permute-start | bytes 393224 | tf_op jit(solution)/shard_map/ppermute | solution.py:134
Sparse Core Ops, SparseCore 0:
  54.8 128.3 all-gather.2

commit v10 on v9

--- a/solution.py
+++ b/solution.py
@@ -101,7 +101,7 @@
     return row_tiled(right_kernel, (R * K, R * K), R * R, jnp.float32, left_rows, source_rows)
 
 
-def gram_kernel(x_ref, o_ref):
+def gram_kernel(core_ref, x_ref, o_ref):
     tile = x_ref.shape[0]
     rows = x_ref[...].reshape(tile, -1, K)
     gram = jnp.einsum("nik,nil->nkl", rows, rows, preferred_element_type=jnp.float32)
@@ -110,21 +110,26 @@
         o_ref[dst * part : (dst + 1) * part] = gram[c * part : (c + 1) * part]
 
 
-def local_gram(basis_rows):
+def local_gram(basis_rows, core):
     count, width = basis_rows.shape
-    tile = 32 if count % 32 == 0 else count
+    tile = count // 2
     return pl.pallas_call(
         gram_kernel,
-        grid=(count // tile,),
-        in_specs=[pl.BlockSpec((tile, width), lambda i: (i, 0))],
-        out_specs=pl.BlockSpec((tile, K, K), lambda i: (i, 0, 0)),
+        grid_spec=pltpu.PrefetchScalarGridSpec(
+            num_scalar_prefetch=1,
+            grid=(2,),
+            in_specs=[pl.BlockSpec((tile, width), lambda i, c: (i, 0))],
+            out_specs=pl.BlockSpec((tile, K, K), lambda i, c: ((i + c[0]) % 2, 0, 0)),
+        ),
         out_shape=jax.ShapeDtypeStruct((count, K, K), jnp.float32),
-    )(basis_rows)
+    )(core.reshape(1), basis_rows)
 
 
 def halving_scatter(x):
     coup_size = lax.axis_size("coup")
-    steps = [("basis", 1)] + [("coup", bit) for bit in (1, 2) if bit < coup_size]
+    half = x.shape[0] // 2
+    x = x[:half] + lax.ppermute(x[half:], "basis", [(0, 1), (1, 0)])
+    steps = [("coup", bit) for bit in (1, 2) if bit < coup_size]
     for axis, bit in steps:
         size = lax.axis_size(axis)
         mine = (lax.axis_index(axis) // bit) % 2
@@ -136,7 +141,7 @@
 
 
 def per_device(basis_rows, transfer, omega, blocks, block_target, source_leaf, source_offset):
-    partial_gram = local_gram(basis_rows)
+    partial_gram = local_gram(basis_rows, lax.axis_index("basis").astype(jnp.int32))
     gram_share = halving_scatter(partial_gram)
     group = lax.axis_size(("basis", "coup"))
     member = lax.axis_index(("basis", "coup"))

time: 216 us -> 216 us (level)
    ppermute x0 -> x1, starting transfers between devices: none -> 3.29 us  [halving_scatter(): x = x[:half] + lax.ppermute(x[half:], 'basis', [(0, 1), (1, 0)])]
    ppermute x3 -> x2, starting transfers between devices: 4.85 us -> 1.57 us  [halving_scatter(): x = keep + lax.ppermute(send, axis, [(i, i ^ bit) for i in range(size)])]
    ppermute x3 -> x2, waiting for transfers between devices: 18.5 us -> 17.1 us  [halving_scatter(): x = keep + lax.ppermute(send, axis, [(i, i ^ bit) for i in range(size)])]
where the time goes in v10:
time: 216 us; the launch traced here: 215 us
  waiting for transfers between devices  105 us (49%)
  Pallas kernels  37.9 us (18%)
  local copies, waits for them, and re-layouts  25.4 us (12%)
  blocking collectives  24.5 us (11%)
  between operations  13.7 us (6%)
  starting transfers between devices  4.86 us (2%)
  other arithmetic  2.65 us (1%)
    all_gather x1, waiting for transfers between devices, per_device(): lax.all_gather(padded_table, ('leaf', 'basis', 'coup'), axis=0, tiled=True)  86.7 us
    all_gather x1, blocking collectives, per_device(): lax.all_gather(local_table, ('basis', 'coup'), axis=0, tiled=True)  24.5 us
    pallas_call x2, Pallas kernels, row_tiled(): pl.pallas_call(kernel, grid=(count // tile,), in_specs=[pl.BlockSpec((til...  21.8 us
    ppermute x2, waiting for transfers between devices, halving_scatter(): x = keep + lax.ppermute(send, axis, [(i, i ^ bit) for i in range(size)])  17.1 us
    gather x1, local copies, waits for them, and re-layouts, per_device(): source_rows = gathered[source_index]  15 us
    pallas_call x1, Pallas kernels, chol_basis(): pl.pallas_call(chol_kernel, out_shape=jax.ShapeDtypeStruct((padded, R * K...  11.5 us
    pallas_call x1, Pallas kernels, local_gram(): pl.pallas_call(gram_kernel, grid_spec=pltpu.PrefetchScalarGridSpec(num_sc...  4.62 us
  transfers between devices with their start and end apart: 4, of which 4 were waited for; matrix products, arithmetic and copies ran while one was open for 4% of the time, Pallas kernels for 5%

profile of v10, /device:TPU:1, one launch (start us, length us, event | category | flops | bytes accessed | tf_op | source)
XLA Modules:
  0.0 215.3 jit_solution(14966419268670033632)
XLA Ops:
  6.5 0.0 copy-start
  6.5 0.0 all-gather.3.cloned.1.call-start
  6.5 4.6 %shard_map.73 = f32[64,64,64]{2,1,0:T(8,128)} custom-call(s32[1]{0:T(128)} %bitcast.core_ref, bf16[64,16384]{1,0:T(8,128)(2,1)} %x_ref.1), custom_call_target="tpu_custom_call" | custom-call | tf_op jit(solution)/shard_map/pallas_call | solution.py:116
  11.2 1.3 slice.39
  12.5 3.3 %collective-permute-start = (f32[32,64,64]{2,1,0:T(8,128)S(1)}, f32[32,64,64]{2,1,0:T(8,128)S(1)}, u32[]{:S(2)}, u32[]{:S(2)}) collective-permute-start(f32[32,64,64]{2,1,0:T(8,128)S(1)} %slice.39), channel_id=1, source_target_pairs={{0,4},{4,0},{1,5},{5,1},{2,6},{6,2},{3,7},{7,3},{8,12},{12,8},{9,1... | collective-permute-start | bytes 1572872 | tf_op jit(solution)/shard_map/ppermute | solution.py:131
  15.8 0.0 copy-done
  15.8 0.8 constant_dynamic-slice_fusion.1
  16.6 1.4 collective-permute-done
  18.1 1.4 slice_add_fusion
  19.5 0.1 collective-permute-start.1
  19.6 0.8 constant_dynamic-slice_fusion
  20.4 0.1 slice.29
  20.6 0.2 slice.28
  20.8 0.8 constant_dynamic-slice_fusion.2
  21.5 11.2 %collective-permute-done.1 = f32[16,64,64]{2,1,0:T(8,128)S(1)} collective-permute-done((f32[16,64,64]{2,1,0:T(8,128)S(1)}, f32[16,64,64]{2,1,0:T(8,128)S(1)}, u32[]{:S(2)}, u32[]{:S(2)}) %collective-permute-start.1) | collective-permute-done | bytes 262176 | tf_op jit(solution)/shard_map/ppermute | solution.py:139
  32.7 0.1 dynamic-slice_add_fusion
  32.8 0.0 copy-start.3
  32.8 0.0 copy-start.1
  32.8 0.0 copy-start.2
  32.9 1.5 collective-permute-start.2
  34.4 0.2 reshape.36
  34.5 0.9 copy.13
  35.4 5.9 %collective-permute-done.2 = f32[8,64,64]{2,1,0:T(8,128)S(1)} collective-permute-done((f32[8,64,64]{2,1,0:T(8,128)S(1)}, f32[8,64,64]{2,1,0:T(8,128)S(1)}, u32[]{:S(2)}, u32[]{:S(2)}) %collective-permute-start.2) | collective-permute-done | bytes 131104 | tf_op jit(solution)/shard_map/ppermute | solution.py:139
  41.3 0.3 fusion.10
  41.6 0.3 bitcast_reduce_fusion
  41.9 0.3 fusion.11
  42.2 0.2 bitcast_reduce_fusion.1
  42.4 0.8 pad_maximum_fusion.g_ref
  43.2 11.5 %shard_map.74 = bf16[16,2048]{1,0:T(8,128)(2,1)} custom-call(f32[14,64,64]{2,1,0:T(8,128)} %pad_maximum_fusion.g_ref, f32[14,32,64]{2,1,0:T(8,128)} %bitcast.18), custom_call_target="tpu_custom_call" | custom-call | tf_op jit(solution)/shard_map/pallas_call | solution.py:59
  54.7 0.0 all-gather.3.cloned.1.call-update
  54.7 0.0 copy-done.3
  54.7 0.0 copy-done.1
  54.7 0.0 copy-done.2
  54.7 0.3 compare_select_fusion
  55.0 0.8 slice_bitcast_fusion.1
  55.9 24.5 %all-gather = bf16[8,14,2048]{2,1,0:T(8,128)(2,1)S(1)} all-gather(bf16[1,14,2048]{2,1,0:T(8,128)(2,1)S(1)} %slice_bitcast_fusion.1), channel_id=1, replica_groups=mesh['leaf'=32,'basis'=2,'coup'=4] {'basis','coup'}, dimensions={0}, use_global_device_ids=true | all-gather | bytes 516096 | tf_op jit(solution)/shard_map/all_gather | solution.py:170
  80.4 0.1 slice.43
  80.7 4.2 %gather_fusion = bf16[768,2048]{1,0:T(8,128)(2,1)} fusion(bf16[112,2048]{1,0:T(8,128)(2,1)S(1)} %pad_maximum_fusion.1, s32[1024]{0:T(1024)S(1)} %pad_clamp_fusion.1), kind=kCustom, calls=%fused_computation | custom fusion | bytes 6294528 | tf_op jit(solution)/shard_map/gather | solution.py:181
  84.9 11.6 %shard_map.75.l_ref = bf16[768,2048]{1,0:T(8,128)(2,1)} custom-call(bf16[768,2048]{1,0:T(8,128)(2,1)} %gather_fusion, bf16[768,4096]{1,0:T(8,128)(2,1)} %s_ref.1), custom_call_target="tpu_custom_call" | custom-call | tf_op jit(solution)/shard_map/pallas_call | solution.py:87
  96.5 86.7 %all-gather.3.cloned.1.call-done = bf16[4096,2048]{1,0:T(8,128)(2,1)} async-done(((bf16[16,2048]{1,0:T(8,128)(2,1)}), bf16[4096,2048]{1,0:T(8,128)(2,1)}) %all-gather.3.cloned.1.call-update) | async-done | bytes 16777232 | tf_op jit(solution)/shard_map/all_gather | solution.py:188
  183.2 15.0 %gather_fusion.1 = bf16[768,2048]{1,0:T(8,128)(2,1)} fusion(bf16[4096,2048]{1,0:T(8,128)(2,1)} %all-gather.3.cloned.1.call-done, s32[1024]{0:T(1024)S(1)} %pad_clamp_fusion), kind=kCustom, calls=%fused_computation.1 | custom fusion | bytes 6294528 | tf_op jit(solution)/shard_map/gather | solution.py:189
  198.3 10.2 %shard_map.76 = f32[768,1024]{1,0:T(8,128)} custom-call(bf16[768,2048]{1,0:T(8,128)(2,1)} %shard_map.75.l_ref, bf16[768,2048]{1,0:T(8,128)(2,1)} %gather_fusion.1), custom_call_target="tpu_custom_call" | custom-call | tf_op jit(solution)/shard_map/pallas_call | solution.py:87
  (14 shorter events, 0.3 us)
Async XLA Ops:
  6.5 9.2 %copy-start = (bf16[96,4096]{1,0:T(8,128)(2,1)S(1)}, bf16[96,4096]{1,0:T(8,128)(2,1)}, u32[]{:S(2)}) copy-start(bf16[96,4096]{1,0:T(8,128)(2,1)} %param.8) | copy-start | bytes 2359300
  6.5 176.7 %all-gather.3.cloned.1.call-start = ((), (), s32[]{:S(2)}) async-start(), calls=%async_computation | async-start | bytes 16842752 | tf_op jit(solution)/shard_map/all_gather | solution.py:188
  12.5 5.6 %collective-permute-start = (f32[32,64,64]{2,1,0:T(8,128)S(1)}, f32[32,64,64]{2,1,0:T(8,128)S(1)}, u32[]{:S(2)}, u32[]{:S(2)}) collective-permute-start(f32[32,64,64]{2,1,0:T(8,128)S(1)} %slice.39), channel_id=1, source_target_pairs={{0,4},{4,0},{1,5},{5,1},{2,6},{6,2},{3,7},{7,3},{8,12},{12,8},{9,1... | collective-permute-start | bytes 1572872 | tf_op jit(solution)/shard_map/ppermute | solution.py:131
  19.5 13.2 %collective-permute-start.1 = (f32[16,64,64]{2,1,0:T(8,128)S(1)}, f32[16,64,64]{2,1,0:T(8,128)S(1)}, u32[]{:S(2)}, u32[]{:S(2)}) collective-permute-start(f32[16,64,64]{2,1,0:T(8,128)S(1)} %constant_dynamic-slice_fusion.6), channel_id=1, source_target_pairs={{0,1},{1,0},{2,3},{3,2},{4,5},{5,4},{6,7},{7,6},{8,9},{9,8},{10,11... | collective-permute-start | bytes 786440 | tf_op jit(solution)/shard_map/ppermute | solution.py:139
  32.8 21.9 %copy-start.3 = (s32[768,1]{0,1:T(1,128)S(1)}, s32[768,1]{0,1:T(1,128)}, u32[]{:S(2)}) copy-start(s32[768,1]{0,1:T(1,128)} %param.12) | copy-start | bytes 9220
  32.8 21.9 %copy-start.1 = (s32[768]{0:T(1024)S(1)}, s32[768]{0:T(1024)}, u32[]{:S(2)}) copy-start(s32[768]{0:T(1024)} %param.13) | copy-start | bytes 9220
  32.8 21.9 %copy-start.2 = (s32[768]{0:T(1024)S(1)}, s32[768]{0:T(1024)}, u32[]{:S(2)}) copy-start(s32[768]{0:T(1024)} %param.11) | copy-start | bytes 9220
  32.9 8.4 %collective-permute-start.2 = (f32[8,64,64]{2,1,0:T(8,128)S(1)}, f32[8,64,64]{2,1,0:T(8,128)S(1)}, u32[]{:S(2)}, u32[]{:S(2)}) collective-permute-start(f32[8,64,64]{2,1,0:T(8,128)S(1)} %constant_dynamic-slice_fusion.5), channel_id=1, source_target_pairs={{0,2},{1,3},{2,0},{3,1},{4,6},{5,7},{6,4},{7,5},{8,10},{9,11},{10,... | collective-permute-start | bytes 393224 | tf_op jit(solution)/shard_map/ppermute | solution.py:139
Sparse Core Ops, SparseCore 0:
  54.8 128.3 all-gather.2
